TPU v7x, 32 devices: a whole 2x2x4 slice. The times are simulated.
32 devices in a mesh: groups: 2 (over y), scan: 4 (over z), depth: 4 (over x, core).
Axes of the slice: x: 2, y: 2, z: 4, core: 2. Of those that a mesh axis runs over, the one named last changes fastest.
Arguments:
- probe: float32 [2, 256, 256], replicated, may hold values from -6 to 6
- slices: float32 [8, 2, 2048, 1024], P('depth', None, ('groups', 'scan')), parts along dimension 2, may hold values from -3 to 3, as said below
- positions: int32 [16, 2], P(('groups', 'scan')), parts along dimension 0, may hold values from 0 to 768, as said below
- counts: int32 [8], P(('groups', 'scan')), parts along dimension 0, may hold values from 1 to 2, as said below
- amplitude: float32 [16, 256, 256], P(('groups', 'scan')), parts along dimension 0, may hold values from 0.2 to 3
Outputs:
- gradient: float32 [8, 2, 2048, 1024], P('depth', None, ('groups', 'scan')), parts along dimension 2
There are 2 independent parts, one for each index of `groups`. A program takes and returns all parts, laid end to end along the dimension named above; an argument that names none is the same for every part. Nothing has to cross between parts.
Inputs may be any that keep to these rules, and one draw needn't show every extreme that they name: `positions`: row offsets lie in 0 to 255 and column offsets in 0 to 768; both ends of both ranges are taken. `counts`: each tile has 1 to 2 live patches, in its first slots; some tile has 2 and some has 1. `slices`: transmission of magnitude between exp(-1) and exp(1).
All inputs are finite; a program needn't handle non-finite values.
Results may differ from a plain program's by a relative error of at most 0.0003.
Values sent between devices are 32-bit elements; how exact they have to be, the bound alone decides.
No kernel may reach another device: no remote copies, remote signals or barrier semaphores. Data moves between devices by JAX's collectives and lax.ppermute only.
A program may use at most 128 MiB of HBM per device.

v0:
```python
import math

import jax
import jax.numpy as jnp
from jax import lax
from jax.sharding import PartitionSpec as P

chirp_rate = 0.25


def shifted(block, axis, distance):
    devices = range(lax.axis_size(axis))
    route = [((i - distance) % len(devices), i) for i in devices]
    return lax.ppermute(block, axis, route)


def passed_along(block, axis, distance):
    devices = range(lax.axis_size(axis))
    route = [(i - distance, i) for i in devices if i - distance in devices]
    return lax.ppermute(block, axis, route)


def make_tables(length):
    index = jnp.arange(length, dtype=jnp.int32)
    product = index[:, None] * index[None, :] % length
    angle = 2.0 * math.pi / length * product.astype(jnp.float32)
    factor = 1.0 / math.sqrt(length)
    table_real = jnp.cos(angle) * factor
    table_imag = -jnp.sin(angle) * factor
    freq = jnp.where(index < length // 2, index, index - length).astype(jnp.float32)
    theta = -math.pi * chirp_rate / length * (freq[:, None] ** 2 + freq[None, :] ** 2)
    return (table_real, table_imag, jnp.cos(theta), jnp.sin(theta))


def left_product(matrix, field):
    return jnp.einsum(
        "jk,...kl->...jl",
        matrix,
        field,
        preferred_element_type=jnp.float32,
        precision=lax.Precision.HIGHEST,
    )


def right_product(field, matrix):
    return jnp.einsum(
        "...jk,kl->...jl",
        field,
        matrix,
        preferred_element_type=jnp.float32,
        precision=lax.Precision.HIGHEST,
    )


def transform(field, tables, forward):
    table_real = tables[0]
    table_imag = tables[1] if forward else -tables[1]
    real_part = field[..., 0, :, :]
    imag_part = field[..., 1, :, :]
    first_real = left_product(table_real, real_part) - left_product(table_imag, imag_part)
    first_imag = left_product(table_real, imag_part) + left_product(table_imag, real_part)
    out_real = right_product(first_real, table_real) - right_product(first_imag, table_imag)
    out_imag = right_product(first_real, table_imag) + right_product(first_imag, table_real)
    return jnp.stack([out_real, out_imag], axis=-3)


def complex_product(first, second, conjugate):
    first_real = first[..., 0, :, :]
    first_imag = first[..., 1, :, :]
    if conjugate:
        first_imag = -first_imag
    second_real = second[..., 0, :, :]
    second_imag = second[..., 1, :, :]
    return jnp.stack(
        [
            first_real * second_real - first_imag * second_imag,
            first_real * second_imag + first_imag * second_real,
        ],
        axis=-3,
    )


def propagate(field, tables, forward):
    spectrum = transform(field, tables, True)
    sine = tables[3] if forward else -tables[3]
    chirp = jnp.stack([tables[2], sine], axis=0)
    return transform(complex_product(spectrum, chirp, False), tables, False)


def far_field(exit_wave, measured, live, tables):
    spectrum = transform(exit_wave, tables, True)
    power = spectrum[..., 0, :, :] ** 2 + spectrum[..., 1, :, :] ** 2
    keep = live[:, None, None] * (1.0 - measured / jnp.sqrt(power + 1.0))
    residual = spectrum * keep[..., None, :, :]
    return transform(residual, tables, False)


def forward_local(wave_in, windows, tables):
    saved = []
    for layer in range(windows.shape[1]):
        psi = propagate(wave_in, tables, True)
        saved.append(psi)
        wave_in = complex_product(psi, windows[:, layer], False)
    return (wave_in, jnp.stack(saved, axis=1))


def adjoint_local(chi_wave, windows, saved, tables):
    terms = [None] * windows.shape[1]
    for layer in range(windows.shape[1] - 1, -1, -1):
        terms[layer] = complex_product(saved[:, layer], chi_wave, True)
        back = complex_product(windows[:, layer], chi_wave, True)
        chi_wave = propagate(back, tables, False)
    return (chi_wave, jnp.stack(terms, axis=1))


def body(probe, slices, positions, counts, amplitude):
    patch = probe.shape[-1]
    slots = positions.shape[0]
    layers = slices.shape[0]
    tables = make_tables(patch)
    depth_index = lax.axis_index("depth")
    depth_count = lax.axis_size("depth")
    last_group = depth_count - 1
    neighbour = shifted(slices, "scan", -1)
    extended = jnp.concatenate([slices, neighbour], axis=2)

    def cut_window(offset):
        zero = jnp.zeros((), jnp.int32)
        return lax.dynamic_slice(
            extended, (zero, zero, offset[0], offset[1]), (layers, 2, patch, patch)
        )

    windows = jax.vmap(cut_window)(positions)
    live = (jnp.arange(slots, dtype=jnp.int32) < counts[0]).astype(jnp.float32)
    wave_shape = (slots, 2, patch, patch)
    wave_now = jnp.broadcast_to(probe, wave_shape)
    saved = jnp.zeros((slots, layers, 2, patch, patch), jnp.float32)
    for step_number in range(depth_count):

        def advance(state):
            return forward_local(state[0], windows, tables)

        def passing(state):
            return state

        wave_now, saved = lax.cond(depth_index == step_number, advance, passing, (wave_now, saved))
        if step_number < depth_count - 1:
            wave_now = passed_along(wave_now, "depth", 1)
    chi_wave = lax.cond(
        depth_index == last_group,
        lambda waves: far_field(waves, amplitude, live, tables),
        lambda waves: jnp.zeros(wave_shape, jnp.float32),
        wave_now,
    )
    terms = jnp.zeros((slots, layers, 2, patch, patch), jnp.float32)
    for step_number in range(depth_count - 1, -1, -1):

        def retreat(state):
            return adjoint_local(state[0], windows, saved, tables)

        def keeping(state):
            return state

        chi_wave, terms = lax.cond(depth_index == step_number, retreat, keeping, (chi_wave, terms))
        if step_number > 0:
            chi_wave = passed_along(chi_wave, "depth", -1)
    grad_ext = jnp.zeros((layers, 2, 2 * patch, slices.shape[3]), jnp.float32)

    def add_slot(slot_index, grad_now):
        zero = jnp.zeros((), jnp.int32)
        start = (zero, zero, positions[slot_index, 0], positions[slot_index, 1])
        current = lax.dynamic_slice(grad_now, start, (layers, 2, patch, patch))
        return lax.dynamic_update_slice(grad_now, current + terms[slot_index], start)

    grad_ext = lax.fori_loop(0, slots, add_slot, grad_ext)
    margin = shifted(grad_ext[:, :, patch:], "scan", 1)
    return grad_ext[:, :, :patch] + margin


def solution(mesh):
    return jax.shard_map(
        body,
        mesh=mesh,
        in_specs=(
            P(),
            P("depth", None, ("groups", "scan"), None),
            P(("groups", "scan"), None),
            P(("groups", "scan")),
            P(("groups", "scan"), None, None),
        ),
        out_specs=P("depth", None, ("groups", "scan"), None),
        check_vma=False,
    )
```

profile of v0, /device:TPU:0, one launch (start us, length us, event | category | flops | bytes accessed | tf_op | source)
XLA Modules:
  0.0 635.0 jit_solution(11234639726278630442)
XLA Ops:
  0.0 5.0 collective-permute-start
  5.1 1.2 copy.243
  6.3 1.0 broadcast_in_dim.7
  7.4 1.1 negate_multiply_fusion
  9.6 85.6 %collective-permute-done = f32[2,2,256,1024]{3,2,1,0:T(8,128)} collective-permute-done((f32[2,2,256,1024]{3,2,1,0:T(8,128)}, f32[2,2,256,1024]{3,2,1,0:T(8,128)}, u32[]{:S(2)}, u32[]{:S(2)}) %collective-permute-start) | collective-permute-done | bytes 4194336 | tf_op jit(solution)/shard_map/ppermute | solution.py:14
  95.2 8.5 %pad_maximum_fusion.16 = f32[2,2,512,1024]{3,2,1,0:T(8,128)} fusion(f32[2,2,256,1024]{3,2,1,0:T(8,128)} %collective-permute-done, f32[2,2,256,1024]{3,2,1,0:T(8,128)} %param.26), kind=kLoop, calls=%fused_computation.883 | loop fusion | flops 2097152 | bytes 16777216 | tf_op jit(solution)/shard_map/concatenate | solution.py:125
  103.7 7.0 %while.15 = (s32[]{:T(128)}, f32[2,2,512,1024]{3,2,1,0:T(8,128)}, s32[2,4]{1,0:T(2,128)S(1)}, f32[2,2,2,256,256]{4,3,2,1,0:T(8,128)S(1)}, s32[]{:T(128)}) while((s32[]{:T(128)}, f32[2,2,512,1024]{3,2,1,0:T(8,128)}, s32[2,4]{1,0:T(2,128)S(1)}, f32[2,2,2,256,256]{4,3,2,1,0:T(8,128)S(1)}, s32[]{:T(128)}) %tuple.214), condition=%wide.while_cond, body=%wide.while_body.sunk | while | flops 2 | bytes 2097285 | solution.py:129
  104.3 3.0 bitcast_dynamic-update-slice_fusion.2
  107.9 2.8 bitcast_dynamic-update-slice_fusion.2
  110.7 37.3 %conditional.9 = (f32[2,2,256,256]{3,2,0,1:T(8,128)}, f32[2,2,2,256,256]{4,3,0,2,1:T(8,128)}) conditional(s32[]{:T(128)} %convert_element_type.662, (f32[2,2,256,256]{2,3,0,1:T(8,128)}) %tuple.118, (f32[2,2,256,256]{2,3,0,1:T(8,128)}, f32[256,256]{1,0:T(8,128)S(1)}, f32[256,256]{1,0:T(8,128)S(1)}, f32[256,256]{1,0:T(8,128)S(1)}, ...), branch_computations={%region_0.1_spmd, %region_1.2_spmd} | conditional | flops 12893552640 | bytes 83361840 | solution.py:146
  111.0 1.7 fusion.8
  112.7 1.7 fusion.6
  116.7 1.0 convolution_add_fusion.6
  118.7 1.0 convolution_subtract_fusion.6
  124.8 1.2 fusion.49
  126.1 1.0 convolution_subtract_fusion.4
  127.2 1.1 multiply_add_fusion.1
  132.3 1.0 fusion.31
  133.4 1.0 convolution_add_fusion.2
  134.4 1.0 fusion.37
  135.4 1.0 convolution_subtract_fusion.2
  138.5 1.5 fusion.28
  145.2 1.1 pad_maximum_fusion.1
  146.4 1.5 pad_maximum_fusion
  148.0 2.5 copy.246
  150.5 2.3 collective-permute-start.1
  152.8 1.6 collective-permute-done.1
  154.4 10.7 %conditional.10 = (f32[2,2,2,256,256]{4,3,0,2,1:T(8,128)}, f32[2,2,256,256]{2,3,0,1:T(8,128)}) conditional(s32[]{:T(128)} %convert_element_type.663, (f32[2,2,256,256]{2,3,0,1:T(8,128)}, f32[2,2,2,256,256]{4,3,0,2,1:T(8,128)}) %tuple.88, (f32[2,2,256,256]{2,3,0,1:T(8,128)}, f32[256,256]{1,0:T(8,128)S(1)}, f32[256,256]{1,0:T(8,128)S(1)}, ...), branch_computations={%region_2.3_spmd, %region_3.4_spmd} | conditional | flops 12893552640 | bytes 87556200 | solution.py:146
  165.2 37.6 %collective-permute-start.2 = (f32[2,2,256,256]{2,3,0,1:T(8,128)}, f32[2,2,256,256]{2,3,0,1:T(8,128)}, u32[]{:S(2)}, u32[]{:S(2)}) collective-permute-start(f32[2,2,256,256]{2,3,0,1:T(8,128)} %get-tuple-element.1240), channel_id=1, source_target_pairs={{0,1},{1,2},{2,3},{4,5},{5,6},{6,7},{8,9},{9,10},{10,11},{12,13},{... | collective-permute-start | bytes 3145736 | tf_op jit(solution)/shard_map/ppermute | solution.py:20
  202.8 1.6 collective-permute-done.2
  204.4 9.0 %conditional.11 = (f32[2,2,2,256,256]{4,3,0,2,1:T(8,128)}, f32[2,2,256,256]{2,3,0,1:T(8,128)}) conditional(s32[]{:T(128)} %convert_element_type.664, (f32[2,2,256,256]{2,3,0,1:T(8,128)}, f32[2,2,2,256,256]{4,3,0,2,1:T(8,128)}) %tuple.90, (f32[2,2,256,256]{2,3,0,1:T(8,128)}, f32[256,256]{1,0:T(8,128)S(1)}, f32[256,256]{1,0:T(8,128)S(1)}, ...), branch_computations={%region_4.5_spmd, %region_5.6_spmd} | conditional | flops 12893552640 | bytes 87556200 | solution.py:146
  213.4 12.3 %collective-permute-start.3 = (f32[2,2,256,256]{2,3,0,1:T(8,128)}, f32[2,2,256,256]{2,3,0,1:T(8,128)}, u32[]{:S(2)}, u32[]{:S(2)}) collective-permute-start(f32[2,2,256,256]{2,3,0,1:T(8,128)} %get-tuple-element.1241), channel_id=1, source_target_pairs={{0,1},{1,2},{2,3},{4,5},{5,6},{6,7},{8,9},{9,10},{10,11},{12,13},{... | collective-permute-start | bytes 3145736 | tf_op jit(solution)/shard_map/ppermute | solution.py:20
  227.4 11.3 %conditional.12 = (f32[2,2,256,256]{3,2,0,1:T(8,128)}, f32[2,2,2,256,256]{4,3,0,2,1:T(8,128)}) conditional(s32[]{:T(128)} %convert_element_type.665, (f32[2,2,256,256]{2,3,0,1:T(8,128)}, f32[2,2,2,256,256]{4,3,0,2,1:T(8,128)}) %tuple.92, (f32[2,2,256,256]{2,3,0,1:T(8,128)}, f32[256,256]{1,0:T(8,128)S(1)}, f32[256,256]{1,0:T(8,128)S(1)}, ...), branch_computations={%region_6.7_spmd, %region_7.8_spmd} | conditional | flops 12893552640 | bytes 79167504 | solution.py:146
  227.4 2.5 copy.253
  238.7 11.2 %conditional.13 = (f32[2,2,256,256]{3,2,0,1:T(8,128)}) conditional(s32[]{:T(128)} %convert_element_type.665, () %tuple.86, (f32[2,2,256,256]{3,2,0,1:T(8,128)}, f32[256,256]{1,0:T(8,128)S(1)}, f32[256,256]{1,0:T(8,128)S(1)}, f32[256,256]{1,0:T(8,128)S(1)}, f32[256,256]{1,0:T(8,128)S(1)}, /*index=5*/f32[256,256]{1,0:T(8,128)S(1)}, ...), branch_computations={%region_8.9_spmd, %region_9.10_spmd} | conditional | flops 6445465600 | bytes 39845960 | solution.py:149
  238.7 1.1 broadcast.64
  250.0 17.2 %conditional.14 = (f32[2,2,256,256]{3,2,0,1:T(8,128)}, f32[2,2,2,256,256]{4,3,0,2,1:T(8,128)}) conditional(s32[]{:T(128)} %convert_element_type.665, f32[2,2,256,256]{3,2,0,1:T(8,128)} %get-tuple-element.1499, (f32[2,2,2,256,256]{4,3,2,1,0:T(8,128)S(1)}, f32[2,2,256,256]{3,2,0,1:T(8,128)}, f32[256,256]{1,0:T(8,128)S(1)}, ...), branch_computations={%region_10.11_spmd, %region_11.12_spmd} | conditional | flops 12895911936 | bytes 93323312 | solution.py:164
  250.0 1.5 broadcast.66
  267.1 1.3 collective-permute-start.4
  268.4 51.0 %collective-permute-done.4 = f32[2,2,256,256]{3,2,0,1:T(8,128)} collective-permute-done((f32[2,2,256,256]{3,2,0,1:T(8,128)}, f32[2,2,256,256]{3,2,0,1:T(8,128)}, u32[]{:S(2)}, u32[]{:S(2)}) %collective-permute-start.4) | collective-permute-done | bytes 1048608 | tf_op jit(solution)/shard_map/ppermute | solution.py:20
  319.4 8.8 %conditional.15 = ((f32[2,2,256,256]{3,2,0,1:T(8,128)}, f32[2,2,2,256,256]{4,3,0,2,1:T(8,128)})) conditional(s32[]{:T(128)} %convert_element_type.664, (f32[2,2,256,256]{3,2,0,1:T(8,128)}, f32[2,2,2,256,256]{4,3,0,2,1:T(8,128)}) %tuple.96, (f32[2,2,2,256,256]{4,3,2,1,0:T(8,128)S(1)}, f32[2,2,256,256]{3,2,0,1:T(8,128)}, f32[256,256]{1,0:T(8,128)S(1)}, ...), branch_computations={%region_12.13_spmd, %region_13.14_spmd} | conditional | flops 12895911936 | bytes 89128984 | solution.py:164
  328.2 1.3 collective-permute-start.5
  329.5 15.9 %collective-permute-done.5 = f32[2,2,256,256]{3,2,0,1:T(8,128)} collective-permute-done((f32[2,2,256,256]{3,2,0,1:T(8,128)}, f32[2,2,256,256]{3,2,0,1:T(8,128)}, u32[]{:S(2)}, u32[]{:S(2)}) %collective-permute-start.5) | collective-permute-done | bytes 1048608 | tf_op jit(solution)/shard_map/ppermute | solution.py:20
  345.4 8.8 %conditional.16 = ((f32[2,2,256,256]{3,2,0,1:T(8,128)}, f32[2,2,2,256,256]{4,3,0,2,1:T(8,128)})) conditional(s32[]{:T(128)} %convert_element_type.663, (f32[2,2,256,256]{3,2,0,1:T(8,128)}, f32[2,2,2,256,256]{4,3,0,2,1:T(8,128)}) %tuple.98, (f32[2,2,2,256,256]{4,3,2,1,0:T(8,128)S(1)}, f32[2,2,256,256]{3,2,0,1:T(8,128)}, f32[256,256]{1,0:T(8,128)S(1)}, ...), branch_computations={%region_14.15_spmd, %region_15.16_spmd} | conditional | flops 12895911936 | bytes 89128984 | solution.py:164
  354.1 1.3 collective-permute-start.6
  355.4 118.8 %collective-permute-done.6 = f32[2,2,256,256]{3,2,0,1:T(8,128)} collective-permute-done((f32[2,2,256,256]{3,2,0,1:T(8,128)}, f32[2,2,256,256]{3,2,0,1:T(8,128)}, u32[]{:S(2)}, u32[]{:S(2)}) %collective-permute-start.6) | collective-permute-done | bytes 1048608 | tf_op jit(solution)/shard_map/ppermute | solution.py:20
  474.2 22.1 %conditional.17 = (f32[2,2,2,256,256]{4,3,2,1,0:T(8,128)}) conditional(s32[]{:T(128)} %convert_element_type.662, f32[2,2,2,256,256]{4,3,0,2,1:T(8,128)} %get-tuple-element.877, (f32[2,2,2,256,256]{4,3,0,2,1:T(8,128)}, f32[2,2,2,256,256]{4,3,2,1,0:T(8,128)S(1)}, f32[2,2,256,256]{3,2,0,1:T(8,128)}, f32[256,256]{1,0:T(8,128)S(1)}, ...), branch_computations={%region_16.17_spmd, %region_17.18_spmd} | conditional | flops 6449266688 | bytes 56623112 | solution.py:164
  474.2 1.9 slice_bitcast_fusion.56
  476.2 1.5 multiply_add_fusion.57
  485.8 1.0 fusion.554
  487.9 1.0 fusion.559
  488.9 1.3 fusion.539
  493.2 1.1 subtract_bitcast_fusion.7
  494.5 1.5 copy.503
  496.3 4.4 broadcast_in_dim.6
  500.7 33.3 %while.14 = (s32[]{:T(128)}, f32[2,2,512,1024]{3,2,1,0:T(8,128)}, s32[2,2]{1,0:T(2,128)S(1)}, f32[2,2,2,256,256]{4,3,2,1,0:T(8,128)}, s32[]{:T(128)}, /*index=5*/s32[]{:T(128)}, s32[]{:T(128)}, s32[]{:T(128)}) while((s32[]{:T(128)}, f32[2,2,512,1024]{3,2,1,0:T(8,128)}, s32[2,2]{1,0:T(2,128)S(1)}, f32[2,2,2,256,256]{4,3,2,1,0:T(8,128)}, ...), condition=%wide.region_19.20_spmd, body=%wide.region_18.19_spmd.sunk | while | flops 262152 | bytes 5243077 | solution.py:175
  505.1 2.1 bitcast_add_fusion.2
  507.2 12.2 %dynamic_update_slice.8 = f32[2,2,512,1024]{3,2,1,0:T(8,128)} dynamic-update-slice(f32[2,2,512,1024]{3,2,1,0:T(8,128)} %get-tuple-element.1484, f32[2,2,256,256]{3,2,1,0:T(8,128)S(1)} %bitcast_add_fusion.2, s32[]{:T(128)} %constant.72.clone.1..sunk, s32[]{:T(128)} %constant.72.clone.1..sunk, s32[]{:T(128)S(6)} %select_n.700, s32[]{:T(128)S(6)} %select_n.701) | dynamic-update-slice | bytes 2097156 | tf_op jit(solution)/shard_map/while/body/eval_jaxpr/dynamic_update_slice | solution.py:173
  523.9 1.9 bitcast_add_fusion.2
  525.8 8.2 %dynamic_update_slice.8 = f32[2,2,512,1024]{3,2,1,0:T(8,128)} dynamic-update-slice(f32[2,2,512,1024]{3,2,1,0:T(8,128)} %get-tuple-element.1484, f32[2,2,256,256]{3,2,1,0:T(8,128)S(1)} %bitcast_add_fusion.2, s32[]{:T(128)} %constant.72.clone.1..sunk, s32[]{:T(128)} %constant.72.clone.1..sunk, s32[]{:T(128)S(6)} %select_n.700, s32[]{:T(128)S(6)} %select_n.701) | dynamic-update-slice | bytes 2097156 | tf_op jit(solution)/shard_map/while/body/eval_jaxpr/dynamic_update_slice | solution.py:173
  534.0 2.7 slice.290
  536.7 3.2 collective-permute-start.7
  539.9 91.7 %collective-permute-done.7 = f32[2,2,256,1024]{3,2,1,0:T(8,128)S(1)} collective-permute-done((f32[2,2,256,1024]{3,2,1,0:T(8,128)S(1)}, f32[2,2,256,1024]{3,2,1,0:T(8,128)S(1)}, u32[]{:S(2)}, u32[]{:S(2)}) %collective-permute-start.7) | collective-permute-done | bytes 4194336 | tf_op jit(solution)/shard_map/ppermute | solution.py:14
  631.5 2.9 slice_add_fusion
  (63 shorter events, 36.6 us)
Async XLA Ops:
  0.0 8.4 %copy-start.11 = (s32[2,2]{1,0:T(2,128)S(1)}, s32[2,2]{1,0:T(2,128)}, u32[]{:S(2)}) copy-start(s32[2,2]{1,0:T(2,128)} %param.27) | copy-start | bytes 52
  0.0 95.2 %collective-permute-start = (f32[2,2,256,1024]{3,2,1,0:T(8,128)}, f32[2,2,256,1024]{3,2,1,0:T(8,128)}, u32[]{:S(2)}, u32[]{:S(2)}) collective-permute-start(f32[2,2,256,1024]{3,2,1,0:T(8,128)} %param.26), channel_id=1, source_target_pairs={{4,0},{8,4},{12,8},{0,12},{5,1},{9,5},{13,9},{1,13},{6,2},{10,6},{... | collective-permute-start | bytes 12582920 | tf_op jit(solution)/shard_map/ppermute | solution.py:14
  111.0 3.4 copy-start.1
  150.5 3.9 collective-permute-start.1
  165.2 39.3 %collective-permute-start.2 = (f32[2,2,256,256]{2,3,0,1:T(8,128)}, f32[2,2,256,256]{2,3,0,1:T(8,128)}, u32[]{:S(2)}, u32[]{:S(2)}) collective-permute-start(f32[2,2,256,256]{2,3,0,1:T(8,128)} %get-tuple-element.1240), channel_id=1, source_target_pairs={{0,1},{1,2},{2,3},{4,5},{5,6},{6,7},{8,9},{9,10},{10,11},{12,13},{... | collective-permute-start | bytes 3145736 | tf_op jit(solution)/shard_map/ppermute | solution.py:20
  213.4 14.0 %collective-permute-start.3 = (f32[2,2,256,256]{2,3,0,1:T(8,128)}, f32[2,2,256,256]{2,3,0,1:T(8,128)}, u32[]{:S(2)}, u32[]{:S(2)}) collective-permute-start(f32[2,2,256,256]{2,3,0,1:T(8,128)} %get-tuple-element.1241), channel_id=1, source_target_pairs={{0,1},{1,2},{2,3},{4,5},{5,6},{6,7},{8,9},{9,10},{10,11},{12,13},{... | collective-permute-start | bytes 3145736 | tf_op jit(solution)/shard_map/ppermute | solution.py:20
  267.1 52.3 %collective-permute-start.4 = (f32[2,2,256,256]{3,2,0,1:T(8,128)}, f32[2,2,256,256]{3,2,0,1:T(8,128)}, u32[]{:S(2)}, u32[]{:S(2)}) collective-permute-start(f32[2,2,256,256]{3,2,0,1:T(8,128)} %get-tuple-element.873), channel_id=1, source_target_pairs={{1,0},{2,1},{3,2},{5,4},{6,5},{7,6},{9,8},{10,9},{11,10},{13,12},{... | collective-permute-start | bytes 3145736 | tf_op jit(solution)/shard_map/ppermute | solution.py:20
  328.2 17.2 %collective-permute-start.5 = (f32[2,2,256,256]{3,2,0,1:T(8,128)}, f32[2,2,256,256]{3,2,0,1:T(8,128)}, u32[]{:S(2)}, u32[]{:S(2)}) collective-permute-start(f32[2,2,256,256]{3,2,0,1:T(8,128)} %get-tuple-element.875), channel_id=1, source_target_pairs={{1,0},{2,1},{3,2},{5,4},{6,5},{7,6},{9,8},{10,9},{11,10},{13,12},{... | collective-permute-start | bytes 3145736 | tf_op jit(solution)/shard_map/ppermute | solution.py:20
  354.1 120.1 %collective-permute-start.6 = (f32[2,2,256,256]{3,2,0,1:T(8,128)}, f32[2,2,256,256]{3,2,0,1:T(8,128)}, u32[]{:S(2)}, u32[]{:S(2)}) collective-permute-start(f32[2,2,256,256]{3,2,0,1:T(8,128)} %get-tuple-element.878), channel_id=1, source_target_pairs={{1,0},{2,1},{3,2},{5,4},{6,5},{7,6},{9,8},{10,9},{11,10},{13,12},{... | collective-permute-start | bytes 3145736 | tf_op jit(solution)/shard_map/ppermute | solution.py:20
  496.3 4.4 copy-start.12
  534.0 97.5 %copy-start = (f32[2,2,512,1024]{3,2,1,0:T(8,128)S(1)}, f32[2,2,512,1024]{3,2,1,0:T(8,128)}, u32[]{:S(2)}) copy-start(f32[2,2,512,1024]{3,2,1,0:T(8,128)} %get-tuple-element.879) | copy-start | bytes 25165828
  536.7 94.9 %collective-permute-start.7 = (f32[2,2,256,1024]{3,2,1,0:T(8,128)S(1)}, f32[2,2,256,1024]{3,2,1,0:T(8,128)S(1)}, u32[]{:S(2)}, u32[]{:S(2)}) collective-permute-start(f32[2,2,256,1024]{3,2,1,0:T(8,128)S(1)} %slice.290), channel_id=1, source_target_pairs={{12,0},{0,4},{4,8},{8,12},{13,1},{1,5},{5,9},{9,13},{14,2},{2,6},{... | collective-permute-start | bytes 12582920 | tf_op jit(solution)/shard_map/ppermute | solution.py:14
where the time goes:
time: 640 us; the launch traced here: 635 us
  waiting for transfers between devices  367 us (57%)
  loops' own time  80.7 us (13%)
  starting transfers between devices  64.4 us (10%)
  matrix products  50 us (8%)
  local copies, waits for them, and re-layouts  49.1 us (8%)
  other arithmetic  22.3 us (3%)
    ppermute x6, waiting for transfers between devices, passed_along(): return lax.ppermute(block, axis, route)  190 us
    ppermute x2, waiting for transfers between devices, shifted(): return lax.ppermute(block, axis, route)  177 us
    ppermute x6, starting transfers between devices, passed_along(): return lax.ppermute(block, axis, route)  56.1 us
    another operation x4, loops' own time, body(): lax.cond(depth_index == step_number, retreat, keeping, (chi_wave, terms))  33.7 us
    another operation x4, loops' own time, body(): lax.cond(depth_index == step_number, advance, passing, (wave_now, saved))  29.2 us
    dot_general x24, matrix products, left_product(): jnp.einsum('jk,...kl->...jl', matrix, field, preferred_element_type=jnp.f...  25.5 us
    dot_general x24, matrix products, right_product(): jnp.einsum('...jk,kl->...jl', field, matrix, preferred_element_type=jnp.f...  24.6 us
    dynamic_update_slice x2, local copies, waits for them, and re-layouts, add_slot(): lax.dynamic_update_slice(grad_now, current + terms[slot_index], start)  20.4 us
  transfers between devices with their start and end apart: 8, of which 8 were waited for; matrix products, arithmetic and copies ran while one was open for 1% of the time, Pallas kernels for 0%

commit v1 on v0

--- a/solution.py
+++ b/solution.py
@@ -113,32 +113,79 @@
     return (chi_wave, jnp.stack(terms, axis=1))
 
 
+def cut_columns(block, column, width):
+    zero = jnp.zeros((), jnp.int32)
+    start = (zero,) * (block.ndim - 1) + (column,)
+    return lax.dynamic_slice(block, start, block.shape[:-1] + (width,))
+
+
+def cut_rows(block, row, height):
+    zero = jnp.zeros((), jnp.int32)
+    start = (zero,) * (block.ndim - 2) + (row, zero)
+    return lax.dynamic_slice(block, start, block.shape[:-2] + (height, block.shape[-1]))
+
+
+def add_at_column(target, block, column):
+    zero = jnp.zeros((), jnp.int32)
+    start = (zero,) * (target.ndim - 1) + (column,)
+    current = lax.dynamic_slice(target, start, block.shape)
+    return lax.dynamic_update_slice(target, current + block, start)
+
+
 def body(probe, slices, positions, counts, amplitude):
     patch = probe.shape[-1]
     slots = positions.shape[0]
     layers = slices.shape[0]
+    tile_rows = slices.shape[2]
     tables = make_tables(patch)
     depth_index = lax.axis_index("depth")
     depth_count = lax.axis_size("depth")
     last_group = depth_count - 1
-    neighbour = shifted(slices, "scan", -1)
-    extended = jnp.concatenate([slices, neighbour], axis=2)
-
-    def cut_window(offset):
-        zero = jnp.zeros((), jnp.int32)
-        return lax.dynamic_slice(
-            extended, (zero, zero, offset[0], offset[1]), (layers, 2, patch, patch)
-        )
-
-    windows = jax.vmap(cut_window)(positions)
+    before = shifted(positions, "scan", 1)
+
+    def neighbour_part(layer):
+        parts = [cut_columns(slices[layer, :, :patch], before[b, 1], patch) for b in range(slots)]
+        return shifted(jnp.stack(parts, axis=0), "scan", -1)
+
+    below = [neighbour_part(layer) for layer in range(layers)]
+
+    def window(b, layer):
+        own = cut_columns(slices[layer, :, :patch], positions[b, 1], patch)
+        both = jnp.concatenate([own, below[layer][b]], axis=-2)
+        return cut_rows(both, positions[b, 0], patch)
+
     live = (jnp.arange(slots, dtype=jnp.int32) < counts[0]).astype(jnp.float32)
     wave_shape = (slots, 2, patch, patch)
-    wave_now = jnp.broadcast_to(probe, wave_shape)
+
+    def forward_stage(wave_in, first):
+        saved = []
+        for layer in range(layers):
+            if first and layer == 0:
+                psi = jnp.broadcast_to(propagate(probe[None], tables, True), wave_shape)
+            else:
+                psi = propagate(wave_in, tables, True)
+            saved.append(psi)
+            windows = jnp.stack([window(b, layer) for b in range(slots)], axis=0)
+            wave_in = complex_product(psi, windows, False)
+        return (wave_in, jnp.stack(saved, axis=1))
+
+    def adjoint_stage(chi_wave, saved, first):
+        terms = [None] * layers
+        for layer in range(layers - 1, -1, -1):
+            terms[layer] = complex_product(saved[:, layer], chi_wave, True)
+            if first and layer == 0:
+                continue
+            windows = jnp.stack([window(b, layer) for b in range(slots)], axis=0)
+            back = complex_product(windows, chi_wave, True)
+            chi_wave = propagate(back, tables, False)
+        return (chi_wave, jnp.stack(terms, axis=1))
+
+    wave_now = jnp.zeros(wave_shape, jnp.float32)
     saved = jnp.zeros((slots, layers, 2, patch, patch), jnp.float32)
     for step_number in range(depth_count):
 
-        def advance(state):
-            return forward_local(state[0], windows, tables)
+        def advance(state, first=step_number == 0):
+            return forward_stage(state[0], first)
 
         def passing(state):
             return state
@@ -155,8 +202,8 @@
     terms = jnp.zeros((slots, layers, 2, patch, patch), jnp.float32)
     for step_number in range(depth_count - 1, -1, -1):
 
-        def retreat(state):
-            return adjoint_local(state[0], windows, saved, tables)
+        def retreat(state, first=step_number == 0):
+            return adjoint_stage(state[0], saved, first)
 
         def keeping(state):
             return state
@@ -164,17 +211,17 @@
         chi_wave, terms = lax.cond(depth_index == step_number, retreat, keeping, (chi_wave, terms))
         if step_number > 0:
             chi_wave = passed_along(chi_wave, "depth", -1)
-    grad_ext = jnp.zeros((layers, 2, 2 * patch, slices.shape[3]), jnp.float32)
-
-    def add_slot(slot_index, grad_now):
-        zero = jnp.zeros((), jnp.int32)
-        start = (zero, zero, positions[slot_index, 0], positions[slot_index, 1])
-        current = lax.dynamic_slice(grad_now, start, (layers, 2, patch, patch))
-        return lax.dynamic_update_slice(grad_now, current + terms[slot_index], start)
-
-    grad_ext = lax.fori_loop(0, slots, add_slot, grad_ext)
-    margin = shifted(grad_ext[:, :, patch:], "scan", 1)
-    return grad_ext[:, :, :patch] + margin
+    blank = jnp.zeros(terms.shape[:-2] + (patch, patch), jnp.float32)
+    padded = jnp.concatenate([blank, terms, blank], axis=-2)
+    upper = [cut_rows(padded[b], patch - positions[b, 0], patch) for b in range(slots)]
+    lower = [cut_rows(padded[b], 2 * patch - positions[b, 0], patch) for b in range(slots)]
+    arrived = shifted(jnp.stack(lower, axis=0), "scan", 1)
+    gradient = jnp.zeros((layers, 2, tile_rows, slices.shape[3]), jnp.float32)
+    for b in range(slots):
+        gradient = add_at_column(gradient, upper[b], positions[b, 1])
+    for b in range(slots):
+        gradient = add_at_column(gradient, arrived[b], before[b, 1])
+    return gradient
 
 
 def solution(mesh):

time: 640 us -> 649 us (1.014)
  waiting for transfers between devices: 367 us -> 326 us
  local copies, waits for them, and re-layouts: 49.1 us -> 69.2 us
  starting transfers between devices: 64.4 us -> 83.1 us
  between operations: 1.32 us -> 13.7 us
  loops' own time: 80.7 us -> 90.5 us
    ppermute x2 -> x4, waiting for transfers between devices: 177 us -> 52 us  [shifted(): return lax.ppermute(block, axis, route)]
    ppermute x6, waiting for transfers between devices: 190 us -> 274 us  [passed_along(): return lax.ppermute(block, axis, route)]
    ppermute x6, starting transfers between devices: 56.1 us -> 74.2 us  [passed_along(): return lax.ppermute(block, axis, route)]
    slice x1 -> x8, local copies, waits for them, and re-layouts: 2.65 us -> 13.2 us  [the longest x4 7.15 us: window(): own = cut_columns(slices[layer, :, :patch], positions[b, 1], patch)]
    another operation x4, loops' own time: 29.2 us -> 39.2 us  [body(): lax.cond(depth_index == step_number, advance, passing, (wave_now, saved))]
    dynamic_slice x2 -> x8, local copies, waits for them, and re-layouts: 1.17 us -> 10.7 us  [the longest x6 9.2 us: cut_columns(): return lax.dynamic_slice(block, start, block.shape[:-1] + (width,))]
    concatenate x2 -> x1, other arithmetic: 8.54 us -> 0.55 us  [body(): padded = jnp.concatenate([blank, terms, blank], axis=-2)]
    another operation x2 -> x0, loops' own time: 7.75 us -> none  [the longest x1 7.72 us: body(): grad_ext = lax.fori_loop(0, slots, add_slot, grad_ext)]
  transfers between devices with their start and end apart: 8 -> 10, of which waited for: 8 -> 9; matrix products, arithmetic and copies ran while one was open for 1% -> 4% of each run, Pallas kernels for 0% -> 0%
where the time goes in v1:
time: 649 us; the launch traced here: 643 us
  waiting for transfers between devices  326 us (50%)
  loops' own time  90.5 us (14%)
  starting transfers between devices  83.1 us (13%)
  local copies, waits for them, and re-layouts  69.2 us (11%)
  matrix products  44.8 us (7%)
  other arithmetic  16.6 us (3%)
  between operations  13.7 us (2%)
    ppermute x6, waiting for transfers between devices, passed_along(): return lax.ppermute(block, axis, route)  274 us
    ppermute x6, starting transfers between devices, passed_along(): return lax.ppermute(block, axis, route)  74.2 us
    ppermute x4, waiting for transfers between devices, shifted(): return lax.ppermute(block, axis, route)  52 us
    another operation x4, loops' own time, body(): lax.cond(depth_index == step_number, retreat, keeping, (chi_wave, terms))  41.1 us
    another operation x4, loops' own time, body(): lax.cond(depth_index == step_number, advance, passing, (wave_now, saved))  39.2 us
    dynamic_update_slice x4, local copies, waits for them, and re-layouts, add_at_column(): return lax.dynamic_update_slice(target, current + block, start)  24.5 us
    dot_general x24, matrix products, right_product(): jnp.einsum('...jk,kl->...jl', field, matrix, preferred_element_type=jnp.f...  23.1 us
    dot_general x24, matrix products, left_product(): jnp.einsum('jk,...kl->...jl', matrix, field, preferred_element_type=jnp.f...  21.7 us
  transfers between devices with their start and end apart: 10, of which 9 were waited for; matrix products, arithmetic and copies ran while one was open for 4% of the time, Pallas kernels for 0%

profile of v1, /device:TPU:0, one launch (start us, length us, event | category | flops | bytes accessed | tf_op | source)
XLA Modules:
  0.0 643.5 jit_solution(10181511560181316724)
XLA Ops:
  0.0 3.0 collective-permute-start
  3.0 4.1 fusion.675
  11.9 2.1 constant_dynamic-slice_fusion.5
  14.0 1.1 pad_maximum_fusion.34
  15.1 1.9 collective-permute-start.2
  18.0 2.1 collective-permute-start.1
  20.1 1.1 negate_multiply_fusion
  22.2 19.2 %collective-permute-done.2 = f32[2,2,256,256]{3,2,1,0:T(8,128)S(1)} collective-permute-done((f32[2,2,256,256]{3,2,1,0:T(8,128)}, f32[2,2,256,256]{3,2,1,0:T(8,128)S(1)}, u32[]{:S(2)}, u32[]{:S(2)}) %collective-permute-start.2) | collective-permute-done | bytes 1048608 | tf_op jit(solution)/shard_map/ppermute | solution.py:14
  41.4 21.0 %collective-permute-done.1 = f32[2,2,256,256]{3,2,1,0:T(8,128)S(1)} collective-permute-done((f32[2,2,256,256]{3,2,1,0:T(8,128)}, f32[2,2,256,256]{3,2,1,0:T(8,128)S(1)}, u32[]{:S(2)}, u32[]{:S(2)}) %collective-permute-start.1) | collective-permute-done | bytes 1048608 | tf_op jit(solution)/shard_map/ppermute | solution.py:14
  62.4 60.3 %conditional.9 = (f32[2,2,256,256]{3,2,0,1:T(8,128)}, f32[2,2,2,256,256]{4,3,0,2,1:T(8,128)}) conditional(s32[]{:T(128)} %convert_element_type.662, () %tuple.73, (f32[2,256,256]{2,1,0:T(8,128)}, f32[256,256]{1,0:T(8,128)S(1)}, f32[256,256]{1,0:T(8,128)S(1)}, f32[256,256]{1,0:T(8,128)S(1)}, f32[256,256]{1,0:T(8,128)S(1)}, ...), branch_computations={%region_0.1_spmd, %region_1.2_spmd} | conditional | flops 9671802880 | bytes 109576632 | solution.py:193
  62.6 1.6 fusion.55
  64.2 1.5 fusion.7
  72.5 1.3 convolution_subtract_fusion.4
  73.8 1.8 copy.8
  76.2 1.5 convolution_add_fusion.4
  83.3 4.0 fusion.659
  87.3 1.3 constant_dynamic-slice_fusion.1
  88.6 2.1 copy.9
  90.7 2.1 copy.10
  96.9 1.3 copy.232
  98.2 1.4 slice_bitcast_fusion.1
  112.7 1.5 convolution_subtract_fusion
  116.4 1.5 pad_maximum_fusion
  119.7 1.1 pad_maximum_fusion.1
  122.7 2.5 copy.233
  125.3 2.3 collective-permute-start.3
  127.6 1.6 collective-permute-done.3
  129.2 10.7 %conditional.10 = (f32[2,2,2,256,256]{4,3,0,2,1:T(8,128)}, f32[2,2,256,256]{2,3,0,1:T(8,128)}) conditional(s32[]{:T(128)} %convert_element_type.663, (f32[2,2,256,256]{2,3,0,1:T(8,128)}, f32[2,2,2,256,256]{4,3,0,2,1:T(8,128)}) %tuple.75, (f32[2,2,256,256]{2,3,0,1:T(8,128)}, f32[256,256]{1,0:T(8,128)S(1)}, f32[256,256]{1,0:T(8,128)S(1)}, ...), branch_computations={%region_2.3_spmd, %region_3.4_spmd} | conditional | flops 12894863360 | bytes 121111040 | solution.py:193
  139.9 55.7 %collective-permute-start.4 = (f32[2,2,256,256]{2,3,0,1:T(8,128)}, f32[2,2,256,256]{2,3,0,1:T(8,128)}, u32[]{:S(2)}, u32[]{:S(2)}) collective-permute-start(f32[2,2,256,256]{2,3,0,1:T(8,128)} %get-tuple-element.942), channel_id=1, source_target_pairs={{0,1},{1,2},{2,3},{4,5},{5,6},{6,7},{8,9},{9,10},{10,11},{12,13},{... | collective-permute-start | bytes 3145736 | tf_op jit(solution)/shard_map/ppermute | solution.py:20
  195.6 1.6 collective-permute-done.4
  197.2 9.0 %conditional.11 = (f32[2,2,2,256,256]{4,3,0,2,1:T(8,128)}, f32[2,2,256,256]{2,3,0,1:T(8,128)}) conditional(s32[]{:T(128)} %convert_element_type.664, (f32[2,2,256,256]{2,3,0,1:T(8,128)}, f32[2,2,2,256,256]{4,3,0,2,1:T(8,128)}) %tuple.77, (f32[2,2,256,256]{2,3,0,1:T(8,128)}, f32[256,256]{1,0:T(8,128)S(1)}, f32[256,256]{1,0:T(8,128)S(1)}, ...), branch_computations={%region_4.5_spmd, %region_5.6_spmd} | conditional | flops 12894863360 | bytes 121111040 | solution.py:193
  206.2 12.4 %collective-permute-start.5 = (f32[2,2,256,256]{2,3,0,1:T(8,128)}, f32[2,2,256,256]{2,3,0,1:T(8,128)}, u32[]{:S(2)}, u32[]{:S(2)}) collective-permute-start(f32[2,2,256,256]{2,3,0,1:T(8,128)} %get-tuple-element.943), channel_id=1, source_target_pairs={{0,1},{1,2},{2,3},{4,5},{5,6},{6,7},{8,9},{9,10},{10,11},{12,13},{... | collective-permute-start | bytes 3145736 | tf_op jit(solution)/shard_map/ppermute | solution.py:20
  220.2 11.3 %conditional.12 = (f32[2,2,256,256]{3,2,0,1:T(8,128)}, f32[2,2,2,256,256]{4,3,0,2,1:T(8,128)}) conditional(s32[]{:T(128)} %convert_element_type.665, (f32[2,2,256,256]{2,3,0,1:T(8,128)}, f32[2,2,2,256,256]{4,3,0,2,1:T(8,128)}) %tuple.79, (f32[2,2,256,256]{2,3,0,1:T(8,128)}, f32[256,256]{1,0:T(8,128)S(1)}, f32[256,256]{1,0:T(8,128)S(1)}, ...), branch_computations={%region_6.7_spmd, %region_7.8_spmd} | conditional | flops 12894863360 | bytes 112722328 | solution.py:193
  220.2 2.5 copy.238
  231.5 11.2 %conditional.13 = (f32[2,2,256,256]{3,2,0,1:T(8,128)}) conditional(s32[]{:T(128)} %convert_element_type.665, () %tuple.72, (f32[2,2,256,256]{3,2,0,1:T(8,128)}, f32[256,256]{1,0:T(8,128)S(1)}, f32[256,256]{1,0:T(8,128)S(1)}, f32[256,256]{1,0:T(8,128)S(1)}, f32[256,256]{1,0:T(8,128)S(1)}, /*index=5*/f32[256,256]{1,0:T(8,128)S(1)}, ...), branch_computations={%region_8.9_spmd, %region_9.10_spmd} | conditional | flops 6445465600 | bytes 39845960 | solution.py:196
  231.5 1.1 broadcast.65
  242.7 17.2 %conditional.14 = (f32[2,2,256,256]{3,2,0,1:T(8,128)}, f32[2,2,2,256,256]{4,3,0,2,1:T(8,128)}) conditional(s32[]{:T(128)} %convert_element_type.665, f32[2,2,256,256]{3,2,0,1:T(8,128)} %get-tuple-element.1200, (f32[2,2,256,1024]{3,2,1,0:T(8,128)}, s32[2,2]{1,0:T(2,128)S(1)}, f32[2,2,256,256]{3,2,1,0:T(8,128)S(1)}, ...), branch_computations={%region_10.11_spmd, %region_11.12_spmd} | conditional | flops 12897222656 | bytes 123732352 | solution.py:211
  242.8 1.5 broadcast.67
  259.9 1.3 collective-permute-start.6
  261.2 69.0 %collective-permute-done.6 = f32[2,2,256,256]{3,2,0,1:T(8,128)} collective-permute-done((f32[2,2,256,256]{3,2,0,1:T(8,128)}, f32[2,2,256,256]{3,2,0,1:T(8,128)}, u32[]{:S(2)}, u32[]{:S(2)}) %collective-permute-start.6) | collective-permute-done | bytes 1048608 | tf_op jit(solution)/shard_map/ppermute | solution.py:20
  330.2 8.8 %conditional.15 = ((f32[2,2,256,256]{3,2,0,1:T(8,128)}, f32[2,2,2,256,256]{4,3,0,2,1:T(8,128)})) conditional(s32[]{:T(128)} %convert_element_type.664, (f32[2,2,256,256]{3,2,0,1:T(8,128)}, f32[2,2,2,256,256]{4,3,0,2,1:T(8,128)}) %tuple.83, (f32[2,2,256,1024]{3,2,1,0:T(8,128)}, s32[2,2]{1,0:T(2,128)S(1)}, f32[2,2,256,256]{3,2,1,0:T(8,128)S(1)}, ...), branch_computations={%region_12.13_spmd, %region_13.14_spmd} | conditional | flops 12897222656 | bytes 119538024 | solution.py:211
  339.0 1.3 collective-permute-start.7
  340.3 15.9 %collective-permute-done.7 = f32[2,2,256,256]{3,2,0,1:T(8,128)} collective-permute-done((f32[2,2,256,256]{3,2,0,1:T(8,128)}, f32[2,2,256,256]{3,2,0,1:T(8,128)}, u32[]{:S(2)}, u32[]{:S(2)}) %collective-permute-start.7) | collective-permute-done | bytes 1048608 | tf_op jit(solution)/shard_map/ppermute | solution.py:20
  356.2 8.8 %conditional.16 = ((f32[2,2,256,256]{3,2,0,1:T(8,128)}, f32[2,2,2,256,256]{4,3,0,2,1:T(8,128)})) conditional(s32[]{:T(128)} %convert_element_type.663, (f32[2,2,256,256]{3,2,0,1:T(8,128)}, f32[2,2,2,256,256]{4,3,0,2,1:T(8,128)}) %tuple.85, (f32[2,2,256,1024]{3,2,1,0:T(8,128)}, s32[2,2]{1,0:T(2,128)S(1)}, f32[2,2,256,256]{3,2,1,0:T(8,128)S(1)}, ...), branch_computations={%region_14.15_spmd, %region_15.16_spmd} | conditional | flops 12897222656 | bytes 119538024 | solution.py:211
  365.0 1.3 collective-permute-start.8
  370.3 184.6 %collective-permute-done.8 = f32[2,2,256,256]{3,2,0,1:T(8,128)S(1)} collective-permute-done((f32[2,2,256,256]{3,2,0,1:T(8,128)}, f32[2,2,256,256]{3,2,0,1:T(8,128)S(1)}, u32[]{:S(2)}, u32[]{:S(2)}) %collective-permute-start.8) | collective-permute-done | bytes 1048608 | tf_op jit(solution)/shard_map/ppermute | solution.py:20
  554.9 32.0 %conditional.17 = (f32[2,2,2,256,256]{4,3,2,1,0:T(8,128)S(1)}) conditional(s32[]{:T(128)} %convert_element_type.662, f32[2,2,2,256,256]{4,3,0,2,1:T(8,128)} %get-tuple-element.866, (f32[2,2,2,256,256]{4,3,0,2,1:T(8,128)}, f32[2,2,256,1024]{3,2,1,0:T(8,128)}, s32[2,2]{1,0:T(2,128)S(1)}, f32[2,2,256,256]{3,2,1,0:T(8,128)S(1)}, ...), branch_computations={%region_16.17_spmd, %region_17.18_spmd} | conditional | flops 6449922048 | bytes 79692072 | solution.py:211
  559.4 1.7 slice.529
  561.1 1.3 dynamic-slice_bitcast_fusion.27
  578.9 1.3 fusion.605
  583.2 1.7 slice_bitcast_fusion.56
  584.9 1.1 subtract_bitcast_fusion.7
  588.4 1.4 constant_dynamic-slice_fusion.3
  590.4 1.5 pad_maximum_fusion.32
  591.8 1.9 collective-permute-start.9
  598.6 2.5 broadcast_in_dim.10
  601.2 6.2 dynamic_update_slice.12
  607.4 2.1 bitcast_add_fusion
  609.4 6.3 dynamic_update_slice.13
  615.7 11.7 %collective-permute-done.9 = f32[2,2,2,256,256]{4,3,2,1,0:T(8,128)S(1)} collective-permute-done((f32[2,2,2,256,256]{4,3,2,1,0:T(8,128)}, f32[2,2,2,256,256]{4,3,2,1,0:T(8,128)S(1)}, u32[]{:S(2)}, u32[]{:S(2)}) %collective-permute-start.9) | collective-permute-done | bytes 2097184 | tf_op jit(solution)/shard_map/ppermute | solution.py:14
  627.5 1.7 fusion.648
  629.2 5.7 dynamic_update_slice.14
  634.9 1.7 fusion.647
  636.7 6.3 dynamic_update_slice.15
  (105 shorter events, 49.1 us)
Async XLA Ops:
  0.0 7.2 %collective-permute-start = (s32[2,2]{1,0:T(2,128)}, s32[2,2]{1,0:T(2,128)S(1)}, u32[]{:S(2)}, u32[]{:S(2)}) collective-permute-start(s32[2,2]{1,0:T(2,128)} %param.25), channel_id=1, source_target_pairs={{12,0},{0,4},{4,8},{8,12},{13,1},{1,5},{5,9},{9,13},{14,2},{2,6},{... | collective-permute-start | bytes 56 | tf_op jit(solution)/shard_map/ppermute | solution.py:14
  15.1 47.3 %copy-start.59 = (s32[2,2]{1,0:T(2,128)S(1)}, s32[2,2]{1,0:T(2,128)}, u32[]{:S(2)}) copy-start(s32[2,2]{1,0:T(2,128)} %param.25) | copy-start | bytes 52
  15.1 26.3 %collective-permute-start.2 = (f32[2,2,256,256]{3,2,1,0:T(8,128)}, f32[2,2,256,256]{3,2,1,0:T(8,128)S(1)}, u32[]{:S(2)}, u32[]{:S(2)}) collective-permute-start(f32[2,2,256,256]{3,2,1,0:T(8,128)} %pad_maximum_fusion.34), channel_id=1, source_target_pairs={{4,0},{8,4},{12,8},{0,12},{5,1},{9,5},{13,9},{1,13},{6,2},{10,6},{... | collective-permute-start | bytes 3145736 | tf_op jit(solution)/shard_map/ppermute | solution.py:14
  18.0 44.4 %collective-permute-start.1 = (f32[2,2,256,256]{3,2,1,0:T(8,128)}, f32[2,2,256,256]{3,2,1,0:T(8,128)S(1)}, u32[]{:S(2)}, u32[]{:S(2)}) collective-permute-start(f32[2,2,256,256]{3,2,1,0:T(8,128)} %pad_maximum_fusion.33), channel_id=1, source_target_pairs={{4,0},{8,4},{12,8},{0,12},{5,1},{9,5},{13,9},{1,13},{6,2},{10,6},{... | collective-permute-start | bytes 3145736 | tf_op jit(solution)/shard_map/ppermute | solution.py:14
  62.6 3.8 copy-start.37
  70.6 1.8 copy-start.18
  98.2 1.4 copy-start.40
  98.2 1.5 copy-start.41
  99.6 1.0 copy-start.56
  99.6 1.1 copy-start.57
  115.1 1.1 copy-start.17
  116.4 2.3 copy-start.13
  125.3 3.9 collective-permute-start.3
  139.9 57.3 %collective-permute-start.4 = (f32[2,2,256,256]{2,3,0,1:T(8,128)}, f32[2,2,256,256]{2,3,0,1:T(8,128)}, u32[]{:S(2)}, u32[]{:S(2)}) collective-permute-start(f32[2,2,256,256]{2,3,0,1:T(8,128)} %get-tuple-element.942), channel_id=1, source_target_pairs={{0,1},{1,2},{2,3},{4,5},{5,6},{6,7},{8,9},{9,10},{10,11},{12,13},{... | collective-permute-start | bytes 3145736 | tf_op jit(solution)/shard_map/ppermute | solution.py:20
  206.2 14.0 %collective-permute-start.5 = (f32[2,2,256,256]{2,3,0,1:T(8,128)}, f32[2,2,256,256]{2,3,0,1:T(8,128)}, u32[]{:S(2)}, u32[]{:S(2)}) collective-permute-start(f32[2,2,256,256]{2,3,0,1:T(8,128)} %get-tuple-element.943), channel_id=1, source_target_pairs={{0,1},{1,2},{2,3},{4,5},{5,6},{6,7},{8,9},{9,10},{10,11},{12,13},{... | collective-permute-start | bytes 3145736 | tf_op jit(solution)/shard_map/ppermute | solution.py:20
  259.9 70.3 %collective-permute-start.6 = (f32[2,2,256,256]{3,2,0,1:T(8,128)}, f32[2,2,256,256]{3,2,0,1:T(8,128)}, u32[]{:S(2)}, u32[]{:S(2)}) collective-permute-start(f32[2,2,256,256]{3,2,0,1:T(8,128)} %get-tuple-element.862), channel_id=1, source_target_pairs={{1,0},{2,1},{3,2},{5,4},{6,5},{7,6},{9,8},{10,9},{11,10},{13,12},{... | collective-permute-start | bytes 3145736 | tf_op jit(solution)/shard_map/ppermute | solution.py:20
  339.0 17.2 %collective-permute-start.7 = (f32[2,2,256,256]{3,2,0,1:T(8,128)}, f32[2,2,256,256]{3,2,0,1:T(8,128)}, u32[]{:S(2)}, u32[]{:S(2)}) collective-permute-start(f32[2,2,256,256]{3,2,0,1:T(8,128)} %get-tuple-element.864), channel_id=1, source_target_pairs={{1,0},{2,1},{3,2},{5,4},{6,5},{7,6},{9,8},{10,9},{11,10},{13,12},{... | collective-permute-start | bytes 3145736 | tf_op jit(solution)/shard_map/ppermute | solution.py:20
  365.0 189.9 %collective-permute-start.8 = (f32[2,2,256,256]{3,2,0,1:T(8,128)}, f32[2,2,256,256]{3,2,0,1:T(8,128)S(1)}, u32[]{:S(2)}, u32[]{:S(2)}) collective-permute-start(f32[2,2,256,256]{3,2,0,1:T(8,128)} %get-tuple-element.867), channel_id=1, source_target_pairs={{1,0},{2,1},{3,2},{5,4},{6,5},{7,6},{9,8},{10,9},{11,10},{13,12},{... | collective-permute-start | bytes 3145736 | tf_op jit(solution)/shard_map/ppermute | solution.py:20
  554.9 12.7 %copy-start.14 = (f32[2,2,256,256]{3,2,0,1:T(8,128)}, f32[2,2,256,256]{3,2,0,1:T(8,128)S(1)}, u32[]{:S(2)}) copy-start(f32[2,2,256,256]{3,2,0,1:T(8,128)S(1)} %get-tuple-element.819) | copy-start | bytes 3145732 | tf_op jit(solution)/shard_map/cond
  566.0 1.0 copy-start.42
  566.0 1.2 copy-start.43
  584.8 1.2 copy-start.15
  588.3 2.1 copy-start.2
  591.8 35.6 %collective-permute-start.9 = (f32[2,2,2,256,256]{4,3,2,1,0:T(8,128)}, f32[2,2,2,256,256]{4,3,2,1,0:T(8,128)S(1)}, u32[]{:S(2)}, u32[]{:S(2)}) collective-permute-start(f32[2,2,2,256,256]{4,3,2,1,0:T(8,128)} %pad_maximum_fusion.32), channel_id=1, source_target_pairs={{12,0},{0,4},{4,8},{8,12},{13,1},{1,5},{5,9},{9,13},{14,2},{2,6},{... | collective-permute-start | bytes 6291464 | tf_op jit(solution)/shard_map/ppermute | solution.py:14
  598.6 2.6 copy-start.16

commit v2 on v0

--- a/solution.py
+++ b/solution.py
@@ -95,86 +95,94 @@
     return transform(residual, tables, False)
 
 
-def forward_local(wave_in, windows, tables):
-    saved = []
-    for layer in range(windows.shape[1]):
-        psi = propagate(wave_in, tables, True)
-        saved.append(psi)
-        wave_in = complex_product(psi, windows[:, layer], False)
-    return (wave_in, jnp.stack(saved, axis=1))
-
-
-def adjoint_local(chi_wave, windows, saved, tables):
-    terms = [None] * windows.shape[1]
-    for layer in range(windows.shape[1] - 1, -1, -1):
-        terms[layer] = complex_product(saved[:, layer], chi_wave, True)
-        back = complex_product(windows[:, layer], chi_wave, True)
-        chi_wave = propagate(back, tables, False)
-    return (chi_wave, jnp.stack(terms, axis=1))
+def cut_columns(block, column, width):
+    zero = jnp.zeros((), jnp.int32)
+    start = (zero,) * (block.ndim - 1) + (column,)
+    return lax.dynamic_slice(block, start, block.shape[:-1] + (width,))
+
+
+def cut_rows(block, row, height):
+    zero = jnp.zeros((), jnp.int32)
+    start = (zero,) * (block.ndim - 2) + (row, zero)
+    return lax.dynamic_slice(block, start, block.shape[:-2] + (height, block.shape[-1]))
+
+
+def add_at_column(target, block, column):
+    zero = jnp.zeros((), jnp.int32)
+    start = (zero,) * (target.ndim - 1) + (column,)
+    current = lax.dynamic_slice(target, start, block.shape)
+    return lax.dynamic_update_slice(target, current + block, start)
 
 
 def body(probe, slices, positions, counts, amplitude):
     patch = probe.shape[-1]
     slots = positions.shape[0]
     layers = slices.shape[0]
+    tile_rows = slices.shape[2]
     tables = make_tables(patch)
     depth_index = lax.axis_index("depth")
     depth_count = lax.axis_size("depth")
-    last_group = depth_count - 1
-    neighbour = shifted(slices, "scan", -1)
-    extended = jnp.concatenate([slices, neighbour], axis=2)
-
-    def cut_window(offset):
-        zero = jnp.zeros((), jnp.int32)
-        return lax.dynamic_slice(
-            extended, (zero, zero, offset[0], offset[1]), (layers, 2, patch, patch)
-        )
-
-    windows = jax.vmap(cut_window)(positions)
+    before = shifted(positions, "scan", 1)
+
+    def windows_of(layer):
+        parts = [cut_columns(slices[layer, :, :patch], before[b, 1], patch) for b in range(slots)]
+        below = shifted(jnp.stack(parts, axis=0), "scan", -1)
+        cut = []
+        for b in range(slots):
+            own = cut_columns(slices[layer, :, :patch], positions[b, 1], patch)
+            both = jnp.concatenate([own, below[b]], axis=-2)
+            cut.append(cut_rows(both, positions[b, 0], patch))
+        return jnp.stack(cut, axis=0)
+
+    windows = [windows_of(layer) for layer in range(layers)]
     live = (jnp.arange(slots, dtype=jnp.int32) < counts[0]).astype(jnp.float32)
     wave_shape = (slots, 2, patch, patch)
-    wave_now = jnp.broadcast_to(probe, wave_shape)
-    saved = jnp.zeros((slots, layers, 2, patch, patch), jnp.float32)
+
+    first_psi = jnp.broadcast_to(propagate(probe[None], tables, True), wave_shape)
+    wave_now = None
+    saved = []
     for step_number in range(depth_count):
-
-        def advance(state):
-            return forward_local(state[0], windows, tables)
-
-        def passing(state):
-            return state
-
-        wave_now, saved = lax.cond(depth_index == step_number, advance, passing, (wave_now, saved))
+        psis = []
+        for layer in range(layers):
+            if step_number == 0 and layer == 0:
+                psi = first_psi
+            else:
+                psi = propagate(wave_now, tables, True)
+            psis.append(psi)
+            wave_now = complex_product(psi, windows[layer], False)
+        saved.append(psis)
         if step_number < depth_count - 1:
             wave_now = passed_along(wave_now, "depth", 1)
-    chi_wave = lax.cond(
-        depth_index == last_group,
-        lambda waves: far_field(waves, amplitude, live, tables),
-        lambda waves: jnp.zeros(wave_shape, jnp.float32),
-        wave_now,
-    )
-    terms = jnp.zeros((slots, layers, 2, patch, patch), jnp.float32)
+    chi_wave = far_field(wave_now, amplitude, live, tables)
+    terms = [[None] * layers for _ in range(depth_count)]
     for step_number in range(depth_count - 1, -1, -1):
-
-        def retreat(state):
-            return adjoint_local(state[0], windows, saved, tables)
-
-        def keeping(state):
-            return state
-
-        chi_wave, terms = lax.cond(depth_index == step_number, retreat, keeping, (chi_wave, terms))
+        for layer in range(layers - 1, -1, -1):
+            terms[step_number][layer] = complex_product(saved[step_number][layer], chi_wave, True)
+            if step_number == 0 and layer == 0:
+                continue
+            back = complex_product(windows[layer], chi_wave, True)
+            chi_wave = propagate(back, tables, False)
         if step_number > 0:
             chi_wave = passed_along(chi_wave, "depth", -1)
-    grad_ext = jnp.zeros((layers, 2, 2 * patch, slices.shape[3]), jnp.float32)
-
-    def add_slot(slot_index, grad_now):
-        zero = jnp.zeros((), jnp.int32)
-        start = (zero, zero, positions[slot_index, 0], positions[slot_index, 1])
-        current = lax.dynamic_slice(grad_now, start, (layers, 2, patch, patch))
-        return lax.dynamic_update_slice(grad_now, current + terms[slot_index], start)
-
-    grad_ext = lax.fori_loop(0, slots, add_slot, grad_ext)
-    margin = shifted(grad_ext[:, :, patch:], "scan", 1)
-    return grad_ext[:, :, :patch] + margin
+    gradient = jnp.zeros((layers, 2, tile_rows, slices.shape[3]), jnp.float32)
+    blank = jnp.zeros((2, patch, patch), jnp.float32)
+    layer_grads = []
+    for layer in range(layers - 1, -1, -1):
+        mine = lax.select_n(depth_index, *[terms[k][layer] for k in range(depth_count)])
+        upper = []
+        lower = []
+        for b in range(slots):
+            padded = jnp.concatenate([blank, mine[b], blank], axis=-2)
+            upper.append(cut_rows(padded, patch - positions[b, 0], patch))
+            lower.append(cut_rows(padded, 2 * patch - positions[b, 0], patch))
+        arrived = shifted(jnp.stack(lower, axis=0), "scan", 1)
+        grad = jnp.zeros((2, tile_rows, slices.shape[3]), jnp.float32)
+        for b in range(slots):
+            grad = add_at_column(grad, upper[b], positions[b, 1])
+        for b in range(slots):
+            grad = add_at_column(grad, arrived[b], before[b, 1])
+        layer_grads.append(grad)
+    return jnp.stack(layer_grads[::-1], axis=0)
 
 
 def solution(mesh):

time: 640 us -> 747 us (1.17)
  the two profiles are of different devices: /device:TPU:0 before, /device:TPU:2 now
where the time goes in v2:
time: 747 us; the launch traced here: 742 us
  matrix products  490 us (66%)
  waiting for transfers between devices  122 us (16%)
  local copies, waits for them, and re-layouts  48.4 us (6%)
  other arithmetic  37 us (5%)
  starting transfers between devices  23.3 us (3%)
  between operations  20.4 us (3%)
    dot_general x128, matrix products, left_product(): jnp.einsum('jk,...kl->...jl', matrix, field, preferred_element_type=jnp.f...  246 us
    dot_general x128, matrix products, right_product(): jnp.einsum('...jk,kl->...jl', field, matrix, preferred_element_type=jnp.f...  244 us
    ppermute x6, waiting for transfers between devices, passed_along(): return lax.ppermute(block, axis, route)  73.7 us
    ppermute x5, waiting for transfers between devices, shifted(): return lax.ppermute(block, axis, route)  48.8 us
    dynamic_update_slice x8, local copies, waits for them, and re-layouts, add_at_column(): return lax.dynamic_update_slice(target, current + block, start)  33.8 us
    ppermute x6, starting transfers between devices, passed_along(): return lax.ppermute(block, axis, route)  15.5 us
  transfers between devices with their start and end apart: 11, of which 10 were waited for; matrix products, arithmetic and copies ran while one was open for 8% of the time, Pallas kernels for 0%

profile of v2, /device:TPU:2, one launch (start us, length us, event | category | flops | bytes accessed | tf_op | source)
XLA Modules:
  0.0 741.9 jit_solution(14906416161699011122)
XLA Ops:
  5.6 2.3 fusion.459
  7.9 2.3 fusion.460
  18.5 2.8 fusion.463
  21.3 2.5 fusion.461
  25.4 2.5 fusion.67
  28.0 2.2 fusion.527
  30.2 3.2 fusion.66
  39.1 3.5 dynamic-slice_bitcast_fusion.7
  42.6 10.1 %pad_maximum_fusion.9 = f32[2,2,256,256]{3,2,1,0:T(8,128)} fusion(f32[1,2,256,256]{3,2,1,0:T(8,128)S(1)} %get-tuple-element.52, f32[1,2,256,256]{3,2,1,0:T(8,128)S(1)} %get-tuple-element.53), kind=kLoop, calls=%fused_computation.205 | loop fusion | flops 262144 | bytes 2097152 | tf_op jit(solution)/shard_map/stack | solution.py:129
  52.8 2.2 collective-permute-start.1
  56.6 2.2 collective-permute-start.2
  66.7 2.2 fusion.1819
  68.9 10.3 %collective-permute-done.1 = f32[2,2,256,256]{3,2,1,0:T(8,128)} collective-permute-done((f32[2,2,256,256]{3,2,1,0:T(8,128)}, f32[2,2,256,256]{3,2,1,0:T(8,128)}, u32[]{:S(2)}, u32[]{:S(2)}) %collective-permute-start.1) | collective-permute-done | bytes 1048608 | tf_op jit(solution)/shard_map/ppermute | solution.py:14
  80.5 19.8 %collective-permute-done.2 = f32[2,2,256,256]{3,2,1,0:T(8,128)} collective-permute-done((f32[2,2,256,256]{3,2,1,0:T(8,128)S(1)}, f32[2,2,256,256]{3,2,1,0:T(8,128)}, u32[]{:S(2)}, u32[]{:S(2)}) %collective-permute-start.2) | collective-permute-done | bytes 1048608 | tf_op jit(solution)/shard_map/ppermute | solution.py:14
  106.9 2.3 fusion.65
  120.3 2.1 fusion.444
  131.7 2.2 convolution_add_fusion.56
  136.7 14.2 %collective-permute-done.3 = f32[2,2,256,256]{3,2,0,1:T(8,128)S(1)} collective-permute-done((f32[2,2,256,256]{3,2,0,1:T(8,128)S(1)}, f32[2,2,256,256]{3,2,0,1:T(8,128)S(1)}, u32[]{:S(2)}, u32[]{:S(2)}) %collective-permute-start.3) | collective-permute-done | bytes 1048608 | tf_op jit(solution)/shard_map/ppermute | solution.py:20
  184.7 2.2 fusion.57
  198.1 2.1 fusion.418
  209.6 2.2 convolution_add_fusion.48
  214.0 14.2 %collective-permute-done.4 = f32[2,2,256,256]{3,2,0,1:T(8,128)S(1)} collective-permute-done((f32[2,2,256,256]{3,2,0,1:T(8,128)S(1)}, f32[2,2,256,256]{3,2,0,1:T(8,128)S(1)}, u32[]{:S(2)}, u32[]{:S(2)}) %collective-permute-start.4) | collective-permute-done | bytes 1048608 | tf_op jit(solution)/shard_map/ppermute | solution.py:20
  250.7 2.1 fusion.156
  262.0 2.2 fusion.49
  275.4 2.1 fusion.392
  286.9 2.2 convolution_add_fusion.40
  292.0 13.5 %collective-permute-done.5 = f32[2,2,256,256]{3,2,0,1:T(8,128)S(1)} collective-permute-done((f32[2,2,256,256]{3,2,0,1:T(8,128)S(1)}, f32[2,2,256,256]{3,2,0,1:T(8,128)S(1)}, u32[]{:S(2)}, u32[]{:S(2)}) %collective-permute-start.5) | collective-permute-done | bytes 1048608 | tf_op jit(solution)/shard_map/ppermute | solution.py:20
  328.0 2.1 fusion.146
  339.4 2.2 fusion.41
  352.8 2.1 fusion.366
  364.2 2.1 multiply_add_fusion.14
  375.5 2.2 fusion.36
  394.7 3.0 subtract_bitcast_fusion
  412.7 2.3 fusion.336
  426.4 3.0 subtract_bitcast_fusion.4
  450.1 2.2 fusion.324
  459.9 2.1 collective-permute-start.6
  462.0 12.1 %collective-permute-done.6 = f32[2,2,256,256]{3,2,0,1:T(8,128)S(1)} collective-permute-done((f32[2,2,256,256]{3,2,0,1:T(8,128)S(1)}, f32[2,2,256,256]{3,2,0,1:T(8,128)S(1)}, u32[]{:S(2)}, u32[]{:S(2)}) %collective-permute-start.6) | collective-permute-done | bytes 1048608 | tf_op jit(solution)/shard_map/ppermute | solution.py:20
  486.5 2.1 convolution_subtract_fusion.18
  497.9 2.2 fusion.312
  503.9 3.0 subtract_bitcast_fusion.5
  523.8 2.3 fusion.300
  537.5 3.8 collective-permute-start.7
  541.3 12.3 %collective-permute-done.7 = f32[2,2,256,256]{3,2,0,1:T(8,128)S(1)} collective-permute-done((f32[2,2,256,256]{3,2,0,1:T(8,128)S(1)}, f32[2,2,256,256]{3,2,0,1:T(8,128)S(1)}, u32[]{:S(2)}, u32[]{:S(2)}) %collective-permute-start.7) | collective-permute-done | bytes 1048608 | tf_op jit(solution)/shard_map/ppermute | solution.py:20
  566.1 2.3 convolution_subtract_fusion.10
  583.5 3.0 subtract_bitcast_fusion.6
  590.2 2.1 fusion.9
  603.4 2.3 fusion.274
  618.1 3.8 collective-permute-start.8
  627.2 7.4 collective-permute-done.8
  647.0 2.2 convolution_subtract_fusion.2
  667.5 2.6 pad_maximum_fusion.3
  670.5 4.5 dynamic_update_slice.26
  675.0 2.2 dynamic-slice_bitcast_fusion.2
  681.2 4.5 dynamic_update_slice.30
  688.5 3.8 dynamic_update_slice.27
  692.3 4.4 dynamic_update_slice.31
  696.7 10.0 %collective-permute-done.9 = f32[2,2,256,256]{3,2,1,0:T(8,128)} collective-permute-done((f32[2,2,256,256]{3,2,1,0:T(8,128)}, f32[2,2,256,256]{3,2,1,0:T(8,128)}, u32[]{:S(2)}, u32[]{:S(2)}) %collective-permute-start.9) | collective-permute-done | bytes 1048608 | tf_op jit(solution)/shard_map/ppermute | solution.py:14
  708.2 3.8 dynamic_update_slice.28
  712.0 8.7 %collective-permute-done.10 = f32[2,2,256,256]{3,2,1,0:T(8,128)} collective-permute-done((f32[2,2,256,256]{3,2,1,0:T(8,128)}, f32[2,2,256,256]{3,2,1,0:T(8,128)}, u32[]{:S(2)}, u32[]{:S(2)}) %collective-permute-start.10) | collective-permute-done | bytes 1048608 | tf_op jit(solution)/shard_map/ppermute | solution.py:14
  721.9 4.5 dynamic_update_slice.32
  728.0 3.8 dynamic_update_slice.29
  733.0 4.5 dynamic_update_slice.33
  737.5 4.2 pad_maximum_fusion
  (330 shorter events, 444.1 us)
Async XLA Ops:
  0.0 10.2 %copy-start.24 = (f32[2,256,256]{2,1,0:T(8,128)S(1)}, f32[2,256,256]{2,1,0:T(8,128)}, u32[]{:S(2)}) copy-start(f32[2,256,256]{2,1,0:T(8,128)} %param.5) | copy-start | bytes 1572868
  0.0 34.7 %collective-permute-start = (s32[2,2]{1,0:T(2,128)}, s32[2,2]{1,0:T(2,128)S(1)}, u32[]{:S(2)}, u32[]{:S(2)}) collective-permute-start(s32[2,2]{1,0:T(2,128)} %param.7), channel_id=1, source_target_pairs={{12,0},{0,4},{4,8},{8,12},{13,1},{1,5},{5,9},{9,13},{14,2},{2,6},{... | collective-permute-start | bytes 56 | tf_op jit(solution)/shard_map/ppermute | solution.py:14
  17.1 6.7 copy-start.4
  28.0 11.2 %copy-start.28 = (f32[256,256]{0,1:T(8,128)}, f32[256,256]{0,1:T(8,128)S(1)}, u32[]{:S(2)}) copy-start(f32[256,256]{0,1:T(8,128)S(1)} %fusion.67) | copy-start | bytes 786436
  52.8 26.4 %collective-permute-start.1 = (f32[2,2,256,256]{3,2,1,0:T(8,128)}, f32[2,2,256,256]{3,2,1,0:T(8,128)}, u32[]{:S(2)}, u32[]{:S(2)}) collective-permute-start(f32[2,2,256,256]{3,2,1,0:T(8,128)} %pad_maximum_fusion.9), channel_id=1, source_target_pairs={{4,0},{8,4},{12,8},{0,12},{5,1},{9,5},{13,9},{1,13},{6,2},{10,6},{... | collective-permute-start | bytes 3145736 | tf_op jit(solution)/shard_map/ppermute | solution.py:14
  56.5 2.3 copy-start.29
  56.5 7.7 %copy-start.26 = (f32[256,256]{0,1:T(8,128)S(1)}, f32[256,256]{0,1:T(8,128)}, u32[]{:S(2)}) copy-start(f32[256,256]{0,1:T(8,128)} %fusion.66) | copy-start | bytes 786436
  56.6 10.1 %copy-start.25 = (f32[256,256]{1,0:T(8,128)S(1)}, f32[256,256]{1,0:T(8,128)}, u32[]{:S(2)}) copy-start(f32[256,256]{1,0:T(8,128)} %fusion.527) | copy-start | bytes 786436
  56.6 10.1 %copy-start.27 = (f32[256,256]{0,1:T(8,128)S(1)}, f32[256,256]{0,1:T(8,128)}, u32[]{:S(2)}) copy-start(f32[256,256]{0,1:T(8,128)} %fusion.66) | copy-start | bytes 786436
  56.6 43.6 %collective-permute-start.2 = (f32[2,2,256,256]{3,2,1,0:T(8,128)S(1)}, f32[2,2,256,256]{3,2,1,0:T(8,128)}, u32[]{:S(2)}, u32[]{:S(2)}) collective-permute-start(f32[2,2,256,256]{3,2,1,0:T(8,128)S(1)} %pad_maximum_fusion.10), channel_id=1, source_target_pairs={{4,0},{8,4},{12,8},{0,12},{5,1},{9,5},{13,9},{1,13},{6,2},{10,6},{... | collective-permute-start | bytes 3145736 | tf_op jit(solution)/shard_map/ppermute | solution.py:14
  68.9 32.7 %copy-start.19 = (f32[2,256,256]{2,1,0:T(8,128)S(1)}, f32[2,256,256]{2,1,0:T(8,128)}, u32[]{:S(2)}) copy-start(f32[2,256,256]{2,1,0:T(8,128)} %get-tuple-element.51) | copy-start | bytes 1572868
  68.9 32.7 %copy-start.21 = (f32[2,256,256]{2,1,0:T(8,128)S(1)}, f32[2,256,256]{2,1,0:T(8,128)}, u32[]{:S(2)}) copy-start(f32[2,256,256]{2,1,0:T(8,128)} %get-tuple-element.55) | copy-start | bytes 1572868
  101.5 1.0 copy-start.18
  101.5 1.2 copy-start.20
  133.9 0.8 copy-start.1
  134.8 16.1 %collective-permute-start.3 = (f32[2,2,256,256]{3,2,0,1:T(8,128)S(1)}, f32[2,2,256,256]{3,2,0,1:T(8,128)S(1)}, u32[]{:S(2)}, u32[]{:S(2)}) collective-permute-start(f32[2,2,256,256]{3,2,0,1:T(8,128)S(1)} %pad_maximum_fusion.11), channel_id=1, source_target_pairs={{0,1},{1,2},{2,3},{4,5},{5,6},{6,7},{8,9},{9,10},{10,11},{12,13},{... | collective-permute-start | bytes 3145736 | tf_op jit(solution)/shard_map/ppermute | solution.py:20
  212.1 16.1 %collective-permute-start.4 = (f32[2,2,256,256]{3,2,0,1:T(8,128)S(1)}, f32[2,2,256,256]{3,2,0,1:T(8,128)S(1)}, u32[]{:S(2)}, u32[]{:S(2)}) collective-permute-start(f32[2,2,256,256]{3,2,0,1:T(8,128)S(1)} %pad_maximum_fusion.12), channel_id=1, source_target_pairs={{0,1},{1,2},{2,3},{4,5},{5,6},{6,7},{8,9},{9,10},{10,11},{12,13},{... | collective-permute-start | bytes 3145736 | tf_op jit(solution)/shard_map/ppermute | solution.py:20
  289.4 16.1 %collective-permute-start.5 = (f32[2,2,256,256]{3,2,0,1:T(8,128)S(1)}, f32[2,2,256,256]{3,2,0,1:T(8,128)S(1)}, u32[]{:S(2)}, u32[]{:S(2)}) collective-permute-start(f32[2,2,256,256]{3,2,0,1:T(8,128)S(1)} %pad_maximum_fusion.13), channel_id=1, source_target_pairs={{0,1},{1,2},{2,3},{4,5},{5,6},{6,7},{8,9},{9,10},{10,11},{12,13},{... | collective-permute-start | bytes 3145736 | tf_op jit(solution)/shard_map/ppermute | solution.py:20
  373.7 5.9 copy-start.22
  459.9 14.2 %collective-permute-start.6 = (f32[2,2,256,256]{3,2,0,1:T(8,128)S(1)}, f32[2,2,256,256]{3,2,0,1:T(8,128)S(1)}, u32[]{:S(2)}, u32[]{:S(2)}) collective-permute-start(f32[2,2,256,256]{3,2,0,1:T(8,128)S(1)} %pad_maximum_fusion.14), channel_id=1, source_target_pairs={{1,0},{2,1},{3,2},{5,4},{6,5},{7,6},{9,8},{10,9},{11,10},{13,12},{... | collective-permute-start | bytes 3145736 | tf_op jit(solution)/shard_map/ppermute | solution.py:20
  537.5 16.1 %collective-permute-start.7 = (f32[2,2,256,256]{3,2,0,1:T(8,128)S(1)}, f32[2,2,256,256]{3,2,0,1:T(8,128)S(1)}, u32[]{:S(2)}, u32[]{:S(2)}) collective-permute-start(f32[2,2,256,256]{3,2,0,1:T(8,128)S(1)} %pad_maximum_fusion.15), channel_id=1, source_target_pairs={{1,0},{2,1},{3,2},{5,4},{6,5},{7,6},{9,8},{10,9},{11,10},{13,12},{... | collective-permute-start | bytes 3145736 | tf_op jit(solution)/shard_map/ppermute | solution.py:20
  615.1 19.5 %copy-start.2 = (f32[2,256,256]{2,1,0:T(8,128)S(1)}, f32[2,256,256]{2,1,0:T(8,128)}, u32[]{:S(2)}) copy-start(f32[2,256,256]{2,1,0:T(8,128)} %copy-done.1) | copy-start | bytes 1572868
  618.1 16.4 %collective-permute-start.8 = (f32[2,2,256,256]{3,2,0,1:T(8,128)}, f32[2,2,256,256]{3,2,0,1:T(8,128)}, u32[]{:S(2)}, u32[]{:S(2)}) collective-permute-start(f32[2,2,256,256]{3,2,0,1:T(8,128)} %pad_maximum_fusion.16), channel_id=1, source_target_pairs={{1,0},{2,1},{3,2},{5,4},{6,5},{7,6},{9,8},{10,9},{11,10},{13,12},{... | collective-permute-start | bytes 3145736 | tf_op jit(solution)/shard_map/ppermute | solution.py:20
  654.9 5.8 copy-start.5
  654.9 5.8 copy-start.6
  654.9 5.8 copy-start.7
  654.9 5.8 copy-start.8
  654.9 5.8 copy-start.9
  654.9 5.8 copy-start.10
  661.2 3.8 copy-start.23
  663.1 3.8 copy-start.11
  663.1 3.8 copy-start.12
  663.1 3.8 copy-start.13
  663.1 3.8 copy-start.14
  663.1 3.8 copy-start.15
  663.1 3.8 copy-start.16
  675.0 3.4 copy-start
  675.0 5.1 copy-start.3
  678.3 28.4 %collective-permute-start.9 = (f32[2,2,256,256]{3,2,1,0:T(8,128)}, f32[2,2,256,256]{3,2,1,0:T(8,128)}, u32[]{:S(2)}, u32[]{:S(2)}) collective-permute-start(f32[2,2,256,256]{3,2,1,0:T(8,128)} %pad_maximum_fusion.18), channel_id=1, source_target_pairs={{12,0},{0,4},{4,8},{8,12},{13,1},{1,5},{5,9},{9,13},{14,2},{2,6},{... | collective-permute-start | bytes 3145736 | tf_op jit(solution)/shard_map/ppermute | solution.py:14
  685.7 1.5 copy-start.17
  688.3 32.4 %collective-permute-start.10 = (f32[2,2,256,256]{3,2,1,0:T(8,128)}, f32[2,2,256,256]{3,2,1,0:T(8,128)}, u32[]{:S(2)}, u32[]{:S(2)}) collective-permute-start(f32[2,2,256,256]{3,2,1,0:T(8,128)} %pad_maximum_fusion.20), channel_id=1, source_target_pairs={{12,0},{0,4},{4,8},{8,12},{13,1},{1,5},{5,9},{9,13},{14,2},{2,6},{... | collective-permute-start | bytes 3145736 | tf_op jit(solution)/shard_map/ppermute | solution.py:14

commit v3 on v2

--- a/solution.py
+++ b/solution.py
@@ -119,7 +119,7 @@
     slots = positions.shape[0]
     layers = slices.shape[0]
     tile_rows = slices.shape[2]
-    tables = make_tables(patch)
+    tables = lax.optimization_barrier(make_tables(patch))
     depth_index = lax.axis_index("depth")
     depth_count = lax.axis_size("depth")
     before = shifted(positions, "scan", 1)

time: 747 us -> 519 us (0.69)
  the two profiles are of different devices: /device:TPU:2 before, /device:TPU:6 now
where the time goes in v3:
time: 519 us; the launch traced here: 511 us
  matrix products  264 us (51%)
  waiting for transfers between devices  124 us (24%)
  local copies, waits for them, and re-layouts  43.1 us (8%)
  starting transfers between devices  30.2 us (6%)
  other arithmetic  30 us (6%)
  between operations  19.6 us (4%)
    dot_general x128, matrix products, right_product(): jnp.einsum('...jk,kl->...jl', field, matrix, preferred_element_type=jnp.f...  133 us
    dot_general x128, matrix products, left_product(): jnp.einsum('jk,...kl->...jl', matrix, field, preferred_element_type=jnp.f...  131 us
    ppermute x6, waiting for transfers between devices, passed_along(): return lax.ppermute(block, axis, route)  73.5 us
    ppermute x5, waiting for transfers between devices, shifted(): return lax.ppermute(block, axis, route)  50.8 us
    dynamic_update_slice x8, local copies, waits for them, and re-layouts, add_at_column(): return lax.dynamic_update_slice(target, current + block, start)  28.2 us
    ppermute x6, starting transfers between devices, passed_along(): return lax.ppermute(block, axis, route)  16.2 us
    ppermute x5, starting transfers between devices, shifted(): return lax.ppermute(block, axis, route)  13.9 us
  transfers between devices with their start and end apart: 11, of which 10 were waited for; matrix products, arithmetic and copies ran while one was open for 8% of the time, Pallas kernels for 0%

profile of v3, /device:TPU:6, one launch (start us, length us, event | category | flops | bytes accessed | tf_op | source)
XLA Modules:
  0.0 511.3 jit_solution(16952129999447640865)
XLA Ops:
  0.0 1.6 collective-permute-start
  3.7 1.3 fusion.458
  5.0 1.3 fusion.459
  12.5 1.3 fusion.547
  15.1 1.3 fusion.546
  16.4 1.6 fusion.529
  23.7 3.4 dynamic-slice_bitcast_fusion.7
  28.1 2.7 collective-permute-start.1
  30.8 1.6 dynamic-slice_bitcast_fusion.5
  33.5 1.9 collective-permute-start.2
  40.7 1.3 fusion.532
  42.0 12.7 %collective-permute-done.1 = f32[2,2,256,256]{3,2,1,0:T(8,128)} collective-permute-done((f32[2,2,256,256]{3,2,1,0:T(8,128)}, f32[2,2,256,256]{3,2,1,0:T(8,128)}, u32[]{:S(2)}, u32[]{:S(2)}) %collective-permute-start.1) | collective-permute-done | bytes 1048608 | tf_op jit(solution)/shard_map/ppermute | solution.py:14
  54.7 1.3 slice_bitcast_fusion.25
  56.0 19.8 %collective-permute-done.2 = f32[2,2,256,256]{3,2,1,0:T(8,128)} collective-permute-done((f32[2,2,256,256]{3,2,1,0:T(8,128)}, f32[2,2,256,256]{3,2,1,0:T(8,128)}, u32[]{:S(2)}, u32[]{:S(2)}) %collective-permute-start.2) | collective-permute-done | bytes 1048608 | tf_op jit(solution)/shard_map/ppermute | solution.py:14
  75.8 1.3 slice_bitcast_fusion.23
  86.7 1.4 fusion.444
  96.1 2.1 collective-permute-start.3
  98.2 14.0 %collective-permute-done.3 = f32[2,2,256,256]{3,2,0,1:T(8,128)S(1)} collective-permute-done((f32[2,2,256,256]{3,2,0,1:T(8,128)S(1)}, f32[2,2,256,256]{3,2,0,1:T(8,128)S(1)}, u32[]{:S(2)}, u32[]{:S(2)}) %collective-permute-start.3) | collective-permute-done | bytes 1048608 | tf_op jit(solution)/shard_map/ppermute | solution.py:20
  136.9 1.4 fusion.418
  145.7 2.1 collective-permute-start.4
  147.8 14.0 %collective-permute-done.4 = f32[2,2,256,256]{3,2,0,1:T(8,128)S(1)} collective-permute-done((f32[2,2,256,256]{3,2,0,1:T(8,128)S(1)}, f32[2,2,256,256]{3,2,0,1:T(8,128)S(1)}, u32[]{:S(2)}, u32[]{:S(2)}) %collective-permute-start.4) | collective-permute-done | bytes 1048608 | tf_op jit(solution)/shard_map/ppermute | solution.py:20
  186.5 1.4 fusion.392
  195.2 2.1 collective-permute-start.5
  198.0 13.4 %collective-permute-done.5 = f32[2,2,256,256]{3,2,0,1:T(8,128)S(1)} collective-permute-done((f32[2,2,256,256]{3,2,0,1:T(8,128)S(1)}, f32[2,2,256,256]{3,2,0,1:T(8,128)S(1)}, u32[]{:S(2)}, u32[]{:S(2)}) %collective-permute-start.5) | collective-permute-done | bytes 1048608 | tf_op jit(solution)/shard_map/ppermute | solution.py:20
  223.6 1.2 fusion.378
  236.1 1.4 fusion.366
  260.3 2.2 subtract_bitcast_fusion
  263.5 1.2 fusion.343
  276.1 1.5 fusion.30
  278.6 2.2 subtract_bitcast_fusion.4
  297.4 1.9 collective-permute-start.6
  299.3 12.3 %collective-permute-done.6 = f32[2,2,256,256]{3,2,0,1:T(8,128)S(1)} collective-permute-done((f32[2,2,256,256]{3,2,0,1:T(8,128)S(1)}, f32[2,2,256,256]{3,2,0,1:T(8,128)S(1)}, u32[]{:S(2)}, u32[]{:S(2)}) %collective-permute-start.6) | collective-permute-done | bytes 1048608 | tf_op jit(solution)/shard_map/ppermute | solution.py:20
  311.6 1.4 subtract_bitcast_fusion.1
  325.3 1.4 fusion.121
  328.7 2.2 subtract_bitcast_fusion.5
  347.5 4.0 collective-permute-start.7
  351.6 12.1 %collective-permute-done.7 = f32[2,2,256,256]{3,2,0,1:T(8,128)S(1)} collective-permute-done((f32[2,2,256,256]{3,2,0,1:T(8,128)S(1)}, f32[2,2,256,256]{3,2,0,1:T(8,128)S(1)}, u32[]{:S(2)}, u32[]{:S(2)}) %collective-permute-start.7) | collective-permute-done | bytes 1048608 | tf_op jit(solution)/shard_map/ppermute | solution.py:20
  363.7 1.4 subtract_bitcast_fusion.2
  377.3 1.4 fusion.111
  380.7 2.2 subtract_bitcast_fusion.6
  400.5 4.0 collective-permute-start.8
  409.2 7.7 %collective-permute-done.8 = f32[2,2,256,256]{3,2,0,1:T(8,128)} collective-permute-done((f32[2,2,256,256]{3,2,0,1:T(8,128)}, f32[2,2,256,256]{3,2,0,1:T(8,128)}, u32[]{:S(2)}, u32[]{:S(2)}) %collective-permute-start.8) | collective-permute-done | bytes 1048608 | tf_op jit(solution)/shard_map/ppermute | solution.py:20
  416.9 1.5 multiply_subtract_fusion.1
  429.6 1.3 fusion.260
  436.7 2.7 pad_maximum_fusion.3
  439.7 2.2 dynamic_update_slice.26
  441.9 2.2 dynamic-slice_bitcast_fusion.2
  445.2 3.8 collective-permute-start.9
  450.1 2.2 dynamic_update_slice.30
  452.3 1.5 dynamic-slice_bitcast_fusion
  454.9 4.1 collective-permute-start.10
  459.0 3.5 dynamic_update_slice.27
  462.4 3.8 dynamic_update_slice.31
  466.2 10.0 %collective-permute-done.9 = f32[2,2,256,256]{3,2,1,0:T(8,128)} collective-permute-done((f32[2,2,256,256]{3,2,1,0:T(8,128)}, f32[2,2,256,256]{3,2,1,0:T(8,128)}, u32[]{:S(2)}, u32[]{:S(2)}) %collective-permute-start.9) | collective-permute-done | bytes 1048608 | tf_op jit(solution)/shard_map/ppermute | solution.py:14
  476.3 1.5 fusion.87
  477.8 3.8 dynamic_update_slice.28
  481.6 8.3 %collective-permute-done.10 = f32[2,2,256,256]{3,2,1,0:T(8,128)} collective-permute-done((f32[2,2,256,256]{3,2,1,0:T(8,128)}, f32[2,2,256,256]{3,2,1,0:T(8,128)}, u32[]{:S(2)}, u32[]{:S(2)}) %collective-permute-start.10) | collective-permute-done | bytes 1048608 | tf_op jit(solution)/shard_map/ppermute | solution.py:14
  489.9 1.2 fusion.84
  491.1 4.5 dynamic_update_slice.32
  495.6 1.5 fusion.86
  497.1 3.7 dynamic_update_slice.29
  500.9 1.2 fusion.83
  502.1 4.5 dynamic_update_slice.33
  506.6 4.2 pad_maximum_fusion
  (343 shorter events, 250.7 us)
Async XLA Ops:
  0.0 6.3 %copy-start.25 = (f32[2,256,256]{2,1,0:T(8,128)S(1)}, f32[2,256,256]{2,1,0:T(8,128)}, u32[]{:S(2)}) copy-start(f32[2,256,256]{2,1,0:T(8,128)} %param.5) | copy-start | bytes 1572868
  0.0 19.3 %collective-permute-start = (s32[2,2]{1,0:T(2,128)}, s32[2,2]{1,0:T(2,128)S(1)}, u32[]{:S(2)}, u32[]{:S(2)}) collective-permute-start(s32[2,2]{1,0:T(2,128)} %param.7), channel_id=1, source_target_pairs={{12,0},{0,4},{4,8},{8,12},{13,1},{1,5},{5,9},{9,13},{14,2},{2,6},{... | collective-permute-start | bytes 56 | tf_op jit(solution)/shard_map/ppermute | solution.py:14
  3.7 3.9 copy-start.35
  11.5 5.0 copy-start.8
  11.9 2.5 copy-start.9
  14.4 0.7 copy-start.11
  28.1 26.6 %collective-permute-start.1 = (f32[2,2,256,256]{3,2,1,0:T(8,128)}, f32[2,2,256,256]{3,2,1,0:T(8,128)}, u32[]{:S(2)}, u32[]{:S(2)}) collective-permute-start(f32[2,2,256,256]{3,2,1,0:T(8,128)} %pad_maximum_fusion.9), channel_id=1, source_target_pairs={{4,0},{8,4},{12,8},{0,12},{5,1},{9,5},{13,9},{1,13},{6,2},{10,6},{... | collective-permute-start | bytes 3145736 | tf_op jit(solution)/shard_map/ppermute | solution.py:14
  32.4 2.9 copy-start.12
  32.4 7.0 %copy-start.10 = (f32[256,256]{1,0:T(8,128)S(1)}, f32[256,256]{1,0:T(8,128)}, u32[]{:S(2)}) copy-start(f32[256,256]{1,0:T(8,128)} %copy-done.9) | copy-start | bytes 786436
  32.4 7.0 %copy-start.31 = (f32[256,256]{1,0:T(8,128)S(1)}, f32[256,256]{1,0:T(8,128)}, u32[]{:S(2)}) copy-start(f32[256,256]{1,0:T(8,128)} %fusion.547) | copy-start | bytes 786436
  32.4 7.7 %copy-start.32 = (f32[256,256]{1,0:T(8,128)S(1)}, f32[256,256]{1,0:T(8,128)}, u32[]{:S(2)}) copy-start(f32[256,256]{1,0:T(8,128)} %fusion.546) | copy-start | bytes 786436
  33.5 42.3 %collective-permute-start.2 = (f32[2,2,256,256]{3,2,1,0:T(8,128)}, f32[2,2,256,256]{3,2,1,0:T(8,128)}, u32[]{:S(2)}, u32[]{:S(2)}) collective-permute-start(f32[2,2,256,256]{3,2,1,0:T(8,128)} %pad_maximum_fusion.10), channel_id=1, source_target_pairs={{4,0},{8,4},{12,8},{0,12},{5,1},{9,5},{13,9},{1,13},{6,2},{10,6},{... | collective-permute-start | bytes 3145736 | tf_op jit(solution)/shard_map/ppermute | solution.py:14
  40.7 43.0 %copy-start.1 = (f32[256,256]{1,0:T(8,128)}, f32[256,256]{1,0:T(8,128)S(1)}, u32[]{:S(2)}) copy-start(f32[256,256]{1,0:T(8,128)S(1)} %convolution_subtract_fusion.60) | copy-start | bytes 786436
  42.0 35.1 %copy-start.28 = (f32[2,256,256]{2,1,0:T(8,128)S(1)}, f32[2,256,256]{2,1,0:T(8,128)}, u32[]{:S(2)}) copy-start(f32[2,256,256]{2,1,0:T(8,128)} %get-tuple-element.59) | copy-start | bytes 1572868
  42.0 35.1 %copy-start.30 = (f32[2,256,256]{2,1,0:T(8,128)S(1)}, f32[2,256,256]{2,1,0:T(8,128)}, u32[]{:S(2)}) copy-start(f32[2,256,256]{2,1,0:T(8,128)} %get-tuple-element.63) | copy-start | bytes 1572868
  77.1 1.0 copy-start.27
  77.1 1.2 copy-start.29
  94.2 1.2 copy-start.3
  95.3 0.8 copy-start.5
  96.1 16.1 %collective-permute-start.3 = (f32[2,2,256,256]{3,2,0,1:T(8,128)S(1)}, f32[2,2,256,256]{3,2,0,1:T(8,128)S(1)}, u32[]{:S(2)}, u32[]{:S(2)}) collective-permute-start(f32[2,2,256,256]{3,2,0,1:T(8,128)S(1)} %pad_maximum_fusion.11), channel_id=1, source_target_pairs={{0,1},{1,2},{2,3},{4,5},{5,6},{6,7},{8,9},{9,10},{10,11},{12,13},{... | collective-permute-start | bytes 3145736 | tf_op jit(solution)/shard_map/ppermute | solution.py:20
  145.7 16.1 %collective-permute-start.4 = (f32[2,2,256,256]{3,2,0,1:T(8,128)S(1)}, f32[2,2,256,256]{3,2,0,1:T(8,128)S(1)}, u32[]{:S(2)}, u32[]{:S(2)}) collective-permute-start(f32[2,2,256,256]{3,2,0,1:T(8,128)S(1)} %pad_maximum_fusion.12), channel_id=1, source_target_pairs={{0,1},{1,2},{2,3},{4,5},{5,6},{6,7},{8,9},{9,10},{10,11},{12,13},{... | collective-permute-start | bytes 3145736 | tf_op jit(solution)/shard_map/ppermute | solution.py:20
  195.2 16.1 %collective-permute-start.5 = (f32[2,2,256,256]{3,2,0,1:T(8,128)S(1)}, f32[2,2,256,256]{3,2,0,1:T(8,128)S(1)}, u32[]{:S(2)}, u32[]{:S(2)}) collective-permute-start(f32[2,2,256,256]{3,2,0,1:T(8,128)S(1)} %pad_maximum_fusion.13), channel_id=1, source_target_pairs={{0,1},{1,2},{2,3},{4,5},{5,6},{6,7},{8,9},{9,10},{10,11},{12,13},{... | collective-permute-start | bytes 3145736 | tf_op jit(solution)/shard_map/ppermute | solution.py:20
  250.0 2.0 copy-start.34
  297.4 14.2 %collective-permute-start.6 = (f32[2,2,256,256]{3,2,0,1:T(8,128)S(1)}, f32[2,2,256,256]{3,2,0,1:T(8,128)S(1)}, u32[]{:S(2)}, u32[]{:S(2)}) collective-permute-start(f32[2,2,256,256]{3,2,0,1:T(8,128)S(1)} %pad_maximum_fusion.14), channel_id=1, source_target_pairs={{1,0},{2,1},{3,2},{5,4},{6,5},{7,6},{9,8},{10,9},{11,10},{13,12},{... | collective-permute-start | bytes 3145736 | tf_op jit(solution)/shard_map/ppermute | solution.py:20
  347.5 16.1 %collective-permute-start.7 = (f32[2,2,256,256]{3,2,0,1:T(8,128)S(1)}, f32[2,2,256,256]{3,2,0,1:T(8,128)S(1)}, u32[]{:S(2)}, u32[]{:S(2)}) collective-permute-start(f32[2,2,256,256]{3,2,0,1:T(8,128)S(1)} %pad_maximum_fusion.15), channel_id=1, source_target_pairs={{1,0},{2,1},{3,2},{5,4},{6,5},{7,6},{9,8},{10,9},{11,10},{13,12},{... | collective-permute-start | bytes 3145736 | tf_op jit(solution)/shard_map/ppermute | solution.py:20
  398.4 18.5 %copy-start.4 = (f32[2,256,256]{2,1,0:T(8,128)S(1)}, f32[2,256,256]{2,1,0:T(8,128)}, u32[]{:S(2)}) copy-start(f32[2,256,256]{2,1,0:T(8,128)} %copy-done.3) | copy-start | bytes 1572868
  398.4 18.5 %copy-start.6 = (f32[2,256,256]{2,1,0:T(8,128)S(1)}, f32[2,256,256]{2,1,0:T(8,128)}, u32[]{:S(2)}) copy-start(f32[2,256,256]{2,1,0:T(8,128)} %copy-done.5) | copy-start | bytes 1572868
  400.5 16.4 %collective-permute-start.8 = (f32[2,2,256,256]{3,2,0,1:T(8,128)}, f32[2,2,256,256]{3,2,0,1:T(8,128)}, u32[]{:S(2)}, u32[]{:S(2)}) collective-permute-start(f32[2,2,256,256]{3,2,0,1:T(8,128)} %pad_maximum_fusion.16), channel_id=1, source_target_pairs={{1,0},{2,1},{3,2},{5,4},{6,5},{7,6},{9,8},{10,9},{11,10},{13,12},{... | collective-permute-start | bytes 3145736 | tf_op jit(solution)/shard_map/ppermute | solution.py:20
  428.5 3.3 copy-start.13
  428.5 3.3 copy-start.14
  428.5 3.3 copy-start.17
  428.6 3.3 copy-start.18
  428.6 3.3 copy-start.21
  428.6 3.3 copy-start.22
  432.3 2.1 copy-start.2
  432.3 2.1 copy-start.33
  434.3 1.2 copy-start.15
  434.4 1.2 copy-start.16
  434.4 1.3 copy-start.19
  434.4 1.5 copy-start.20
  434.4 1.6 copy-start.23
  434.4 1.8 copy-start.24
  441.9 3.4 copy-start
  441.9 7.1 %copy-start.7 = (f32[2,768,256]{2,1,0:T(8,128)S(1)}, f32[2,768,256]{2,1,0:T(8,128)}, u32[]{:S(2)}) copy-start(f32[2,768,256]{2,1,0:T(8,128)} %get-tuple-element.103) | copy-start | bytes 4718596
  445.2 31.0 %collective-permute-start.9 = (f32[2,2,256,256]{3,2,1,0:T(8,128)}, f32[2,2,256,256]{3,2,1,0:T(8,128)}, u32[]{:S(2)}, u32[]{:S(2)}) collective-permute-start(f32[2,2,256,256]{3,2,1,0:T(8,128)} %pad_maximum_fusion.18), channel_id=1, source_target_pairs={{12,0},{0,4},{4,8},{8,12},{13,1},{1,5},{5,9},{9,13},{14,2},{2,6},{... | collective-permute-start | bytes 3145736 | tf_op jit(solution)/shard_map/ppermute | solution.py:14
  452.3 1.5 copy-start.26
  454.9 35.0 %collective-permute-start.10 = (f32[2,2,256,256]{3,2,1,0:T(8,128)}, f32[2,2,256,256]{3,2,1,0:T(8,128)}, u32[]{:S(2)}, u32[]{:S(2)}) collective-permute-start(f32[2,2,256,256]{3,2,1,0:T(8,128)} %pad_maximum_fusion.20), channel_id=1, source_target_pairs={{12,0},{0,4},{4,8},{8,12},{13,1},{1,5},{5,9},{9,13},{14,2},{2,6},{... | collective-permute-start | bytes 3145736 | tf_op jit(solution)/shard_map/ppermute | solution.py:14

commit v4 on v3

--- a/solution.py
+++ b/solution.py
@@ -107,11 +107,13 @@
     return lax.dynamic_slice(block, start, block.shape[:-2] + (height, block.shape[-1]))
 
 
-def add_at_column(target, block, column):
-    zero = jnp.zeros((), jnp.int32)
-    start = (zero,) * (target.ndim - 1) + (column,)
-    current = lax.dynamic_slice(target, start, block.shape)
-    return lax.dynamic_update_slice(target, current + block, start)
+def place_columns(block, column, width):
+    pad = [(0, 0)] * (block.ndim - 1) + [(width, width - block.shape[-1])]
+    return cut_columns(jnp.pad(block, pad), width - column, width)
+
+
+def pick(stack, index):
+    return lax.dynamic_index_in_dim(stack, index, 0, keepdims=False)
 
 
 def body(probe, slices, positions, counts, amplitude):
@@ -119,70 +121,80 @@
     slots = positions.shape[0]
     layers = slices.shape[0]
     tile_rows = slices.shape[2]
+    width = slices.shape[3]
     tables = lax.optimization_barrier(make_tables(patch))
     depth_index = lax.axis_index("depth")
     depth_count = lax.axis_size("depth")
+    last_group = depth_count - 1
+    steps = slots + depth_count - 1
     before = shifted(positions, "scan", 1)
-
-    def windows_of(layer):
-        parts = [cut_columns(slices[layer, :, :patch], before[b, 1], patch) for b in range(slots)]
-        below = shifted(jnp.stack(parts, axis=0), "scan", -1)
-        cut = []
-        for b in range(slots):
-            own = cut_columns(slices[layer, :, :patch], positions[b, 1], patch)
-            both = jnp.concatenate([own, below[b]], axis=-2)
-            cut.append(cut_rows(both, positions[b, 0], patch))
-        return jnp.stack(cut, axis=0)
-
-    windows = [windows_of(layer) for layer in range(layers)]
+    own_rows = slices[:, :, :patch]
+
+    windows = []
+    for b in range(slots):
+        below = shifted(cut_columns(own_rows, before[b, 1], patch), "scan", -1)
+        own = cut_columns(own_rows, positions[b, 1], patch)
+        both = jnp.concatenate([own, below], axis=-2)
+        windows.append(cut_rows(both, positions[b, 0], patch))
+    windows = jnp.stack(windows, axis=0)
     live = (jnp.arange(slots, dtype=jnp.int32) < counts[0]).astype(jnp.float32)
-    wave_shape = (slots, 2, patch, patch)
-
-    first_psi = jnp.broadcast_to(propagate(probe[None], tables, True), wave_shape)
+
+    first_psi = propagate(probe[None], tables, True)[0]
     wave_now = None
     saved = []
-    for step_number in range(depth_count):
+    exits = []
+    for step_number in range(steps):
+        slot = jnp.clip(step_number - depth_index, 0, slots - 1)
+        mine = pick(windows, slot)
         psis = []
         for layer in range(layers):
-            if step_number == 0 and layer == 0:
+            if layer == 0 and step_number == 0:
                 psi = first_psi
+            elif layer == 0:
+                psi = jnp.where(depth_index == 0, first_psi, propagate(wave_now, tables, True))
             else:
                 psi = propagate(wave_now, tables, True)
             psis.append(psi)
-            wave_now = complex_product(psi, windows[layer], False)
-        saved.append(psis)
-        if step_number < depth_count - 1:
+            wave_now = complex_product(psi, mine[layer], False)
+        saved.append(jnp.stack(psis, axis=0))
+        if step_number >= last_group:
+            exits.append(wave_now)
+        if step_number < steps - 1:
             wave_now = passed_along(wave_now, "depth", 1)
-    chi_wave = far_field(wave_now, amplitude, live, tables)
-    terms = [[None] * layers for _ in range(depth_count)]
-    for step_number in range(depth_count - 1, -1, -1):
+    saved = jnp.stack(saved, axis=0)
+    chi_far = far_field(jnp.stack(exits, axis=0), amplitude, live, tables)
+
+    chi_wave = None
+    terms = []
+    for step_number in range(steps):
+        slot = jnp.clip(step_number - last_group + depth_index, 0, slots - 1)
+        mine = pick(windows, slot)
+        psis = pick(saved, jnp.clip(step_number - last_group + 2 * depth_index, 0, steps - 1))
+        start = chi_far[min(step_number, slots - 1)]
+        chi_wave = start if chi_wave is None else jnp.where(depth_index == last_group, start, chi_wave)
+        found = [None] * layers
         for layer in range(layers - 1, -1, -1):
-            terms[step_number][layer] = complex_product(saved[step_number][layer], chi_wave, True)
-            if step_number == 0 and layer == 0:
+            found[layer] = complex_product(psis[layer], chi_wave, True)
+            if layer == 0 and step_number == steps - 1:
                 continue
-            back = complex_product(windows[layer], chi_wave, True)
+            back = complex_product(mine[layer], chi_wave, True)
             chi_wave = propagate(back, tables, False)
-        if step_number > 0:
+        terms.append(jnp.stack(found, axis=0))
+        if step_number < steps - 1:
             chi_wave = passed_along(chi_wave, "depth", -1)
-    gradient = jnp.zeros((layers, 2, tile_rows, slices.shape[3]), jnp.float32)
-    blank = jnp.zeros((2, patch, patch), jnp.float32)
-    layer_grads = []
-    for layer in range(layers - 1, -1, -1):
-        mine = lax.select_n(depth_index, *[terms[k][layer] for k in range(depth_count)])
-        upper = []
-        lower = []
-        for b in range(slots):
-            padded = jnp.concatenate([blank, mine[b], blank], axis=-2)
-            upper.append(cut_rows(padded, patch - positions[b, 0], patch))
-            lower.append(cut_rows(padded, 2 * patch - positions[b, 0], patch))
-        arrived = shifted(jnp.stack(lower, axis=0), "scan", 1)
-        grad = jnp.zeros((2, tile_rows, slices.shape[3]), jnp.float32)
-        for b in range(slots):
-            grad = add_at_column(grad, upper[b], positions[b, 1])
-        for b in range(slots):
-            grad = add_at_column(grad, arrived[b], before[b, 1])
-        layer_grads.append(grad)
-    return jnp.stack(layer_grads[::-1], axis=0)
+    terms = jnp.stack(terms, axis=0)
+
+    blank = jnp.zeros((layers, 2, patch, patch), jnp.float32)
+    gradient = jnp.zeros((layers, 2, tile_rows, width), jnp.float32)
+    for b in range(slots):
+        found = pick(terms, b + last_group - depth_index)
+        padded = jnp.concatenate([blank, found, blank], axis=-2)
+        upper = cut_rows(padded, patch - positions[b, 0], patch)
+        lower = cut_rows(padded, 2 * patch - positions[b, 0], patch)
+        arrived = shifted(lower, "scan", 1)
+        gradient = gradient + place_columns(upper, positions[b, 1], width)
+        gradient = gradient + place_columns(arrived, before[b, 1], width)
+    return gradient
 
 
 def solution(mesh):

time: 519 us -> 368 us (0.71)
  the two profiles are of different devices: /device:TPU:6 before, /device:TPU:1 now
where the time goes in v4:
time: 368 us; the launch traced here: 361 us
  matrix products  144 us (39%)
  waiting for transfers between devices  118 us (32%)
  starting transfers between devices  34.5 us (9%)
  other arithmetic  26.9 us (7%)
  between operations  26.4 us (7%)
  local copies, waits for them, and re-layouts  10.8 us (3%)
    dot_general x160, matrix products, left_product(): jnp.einsum('jk,...kl->...jl', matrix, field, preferred_element_type=jnp.f...  73.3 us
    dot_general x160, matrix products, right_product(): jnp.einsum('...jk,kl->...jl', field, matrix, preferred_element_type=jnp.f...  70.7 us
    ppermute x5, waiting for transfers between devices, shifted(): return lax.ppermute(block, axis, route)  69.3 us
    ppermute x8, waiting for transfers between devices, passed_along(): return lax.ppermute(block, axis, route)  48.6 us
    ppermute x8, starting transfers between devices, passed_along(): return lax.ppermute(block, axis, route)  25.8 us
    ppermute x5, starting transfers between devices, shifted(): return lax.ppermute(block, axis, route)  8.71 us
    another operation x4, other arithmetic, body(): windows = jnp.stack(windows, axis=0)  7.93 us
    add x1, other arithmetic, body(): gradient = gradient + place_columns(arrived, before[b, 1], width)  7.63 us
  transfers between devices with their start and end apart: 13, of which 12 were waited for; matrix products, arithmetic and copies ran while one was open for 6% of the time, Pallas kernels for 0%

profile of v4, /device:TPU:1, one launch (start us, length us, event | category | flops | bytes accessed | tf_op | source)
XLA Modules:
  0.0 360.5 jit_solution(1400870848300478666)
XLA Ops:
  0.0 2.1 collective-permute-start
  2.1 1.1 negate_multiply_fusion
  3.2 1.0 fusion.101
  4.2 1.3 fusion.106
  5.5 1.3 fusion.107
  6.9 1.3 convolution_subtract_fusion.79
  20.2 5.6 %constant_dynamic-slice_fusion.4 = (f32[2,2,256,256]{3,2,1,0:T(8,128)S(1)}, f32[2,2,256,256]{3,2,1,0:T(8,128)}, f32[2,2,256,256]{3,2,1,0:T(8,128)}, f32[2,2,256,256]{3,2,1,0:T(8,128)}) fusion(f32[2,2,256,1024]{3,2,1,0:T(8,128)} %param.6, s32[]{:T(128)S(6)} %select_n.170, s32[]{:T(128)S(6)} %select_n.167, s32[]{:T(128)S(6)} %select_n.166, s32[]{:T(128)S(6)} %select_n.169), kind=kLoop, calls=%fused_computation.557 | loop fusion | bytes 8388624 | tf_op jit(solution)/shard_map/dynamic_slice | solution.py:101
  25.8 2.2 collective-permute-start.2
  32.6 1.7 collective-permute-start.1
  36.7 13.1 %collective-permute-done.2 = f32[2,2,256,256]{3,2,1,0:T(8,128)} collective-permute-done((f32[2,2,256,256]{3,2,1,0:T(8,128)S(1)}, f32[2,2,256,256]{3,2,1,0:T(8,128)}, u32[]{:S(2)}, u32[]{:S(2)}) %collective-permute-start.2) | collective-permute-done | bytes 1048608 | tf_op jit(solution)/shard_map/ppermute | solution.py:14
  49.9 1.1 fusion.18
  50.9 21.5 %collective-permute-done.1 = f32[2,2,256,256]{3,2,1,0:T(8,128)S(1)} collective-permute-done((f32[2,2,256,256]{3,2,1,0:T(8,128)}, f32[2,2,256,256]{3,2,1,0:T(8,128)S(1)}, u32[]{:S(2)}, u32[]{:S(2)}) %collective-permute-start.1) | collective-permute-done | bytes 1048608 | tf_op jit(solution)/shard_map/ppermute | solution.py:14
  72.7 2.7 fusion.21
  83.0 0.8 pad_maximum_fusion.7
  83.8 5.1 %collective-permute-start.3 = (f32[2,256,256]{2,1,0:T(8,128)}, f32[2,256,256]{2,1,0:T(8,128)S(1)}, u32[]{:S(2)}, u32[]{:S(2)}) collective-permute-start(f32[2,256,256]{2,1,0:T(8,128)} %pad_maximum_fusion.7), channel_id=1, source_target_pairs={{0,1},{1,2},{2,3},{4,5},{5,6},{6,7},{8,9},{9,10},{10,11},{12,13},{... | collective-permute-start | bytes 1572872 | tf_op jit(solution)/shard_map/ppermute | solution.py:20
  88.9 5.9 %collective-permute-done.3 = f32[2,256,256]{2,1,0:T(8,128)S(1)} collective-permute-done((f32[2,256,256]{2,1,0:T(8,128)}, f32[2,256,256]{2,1,0:T(8,128)S(1)}, u32[]{:S(2)}, u32[]{:S(2)}) %collective-permute-start.3) | collective-permute-done | bytes 524320 | tf_op jit(solution)/shard_map/ppermute | solution.py:20
  107.8 4.3 %collective-permute-start.4 = (f32[2,256,256]{2,1,0:T(8,128)S(1)}, f32[2,256,256]{2,1,0:T(8,128)S(1)}, u32[]{:S(2)}, u32[]{:S(2)}) collective-permute-start(f32[2,256,256]{2,1,0:T(8,128)S(1)} %pad_maximum_fusion.8), channel_id=1, source_target_pairs={{0,1},{1,2},{2,3},{4,5},{5,6},{6,7},{8,9},{9,10},{10,11},{12,13},{... | collective-permute-start | bytes 1572872 | tf_op jit(solution)/shard_map/ppermute | solution.py:20
  112.1 6.1 %collective-permute-done.4 = f32[2,256,256]{2,1,0:T(8,128)S(1)} collective-permute-done((f32[2,256,256]{2,1,0:T(8,128)S(1)}, f32[2,256,256]{2,1,0:T(8,128)S(1)}, u32[]{:S(2)}, u32[]{:S(2)}) %collective-permute-start.4) | collective-permute-done | bytes 524320 | tf_op jit(solution)/shard_map/ppermute | solution.py:20
  131.5 4.4 %collective-permute-start.5 = (f32[2,256,256]{2,1,0:T(8,128)S(1)}, f32[2,256,256]{2,1,0:T(8,128)S(1)}, u32[]{:S(2)}, u32[]{:S(2)}) collective-permute-start(f32[2,256,256]{2,1,0:T(8,128)S(1)} %pad_maximum_fusion.9), channel_id=1, source_target_pairs={{0,1},{1,2},{2,3},{4,5},{5,6},{6,7},{8,9},{9,10},{10,11},{12,13},{... | collective-permute-start | bytes 1572872 | tf_op jit(solution)/shard_map/ppermute | solution.py:20
  135.9 6.1 %collective-permute-done.5 = f32[2,256,256]{2,1,0:T(8,128)S(1)} collective-permute-done((f32[2,256,256]{2,1,0:T(8,128)S(1)}, f32[2,256,256]{2,1,0:T(8,128)S(1)}, u32[]{:S(2)}, u32[]{:S(2)}) %collective-permute-start.5) | collective-permute-done | bytes 524320 | tf_op jit(solution)/shard_map/ppermute | solution.py:20
  155.5 0.9 fusion.126
  156.4 4.4 %collective-permute-start.6 = (f32[2,256,256]{2,1,0:T(8,128)}, f32[2,256,256]{2,1,0:T(8,128)}, u32[]{:S(2)}, u32[]{:S(2)}) collective-permute-start(f32[2,256,256]{2,1,0:T(8,128)} %get-tuple-element.148), channel_id=1, source_target_pairs={{0,1},{1,2},{2,3},{4,5},{5,6},{6,7},{8,9},{9,10},{10,11},{12,13},{... | collective-permute-start | bytes 1572872 | tf_op jit(solution)/shard_map/ppermute | solution.py:20
  161.5 3.9 %fusion.30 = (f32[1,2,2,256,256]{4,3,2,1,0:T(8,128)}, f32[1,2,2,256,256]{4,3,2,1,0:T(8,128)S(1)}, f32[1,2,2,256,256]{4,3,2,1,0:T(8,128)}, f32[1,2,2,256,256]{4,3,2,1,0:T(8,128)}) fusion(s32[]{:T(128)S(6)} %min.58, f32[1,2,2,256,256]{4,3,2,1,0:T(8,128)} %copy-done, f32[1,2,2,256,256]{4,3,2,1,0:T(8,128)S(1)} %fusion.18, s32[]{:T(128)S(6)} %min.52, ...), kind=kLoop, calls=%fused_computation.222 | loop fusion | flops 1048576 | bytes 6291472 | tf_op jit(solution)/shard_map/stack | solution.py:139
  165.4 1.8 collective-permute-done.6
  167.2 1.3 fusion.115
  168.5 1.3 convolution_subtract_fusion.47
  170.7 1.3 fusion.114
  172.0 1.3 convolution_add_fusion.47
  183.0 0.8 convolution_subtract_fusion.40
  184.3 1.0 fusion.99
  185.3 1.0 fusion.95
  186.3 1.0 fusion.6
  187.4 1.0 fusion.84
  188.4 1.0 fusion.97
  189.4 1.0 fusion.5
  190.4 1.0 convolution_subtract_fusion.2
  191.4 1.0 subtract_multiply_fusion
  192.6 1.0 fusion.45
  193.6 1.0 fusion.46
  194.6 1.0 fusion.4
  195.6 1.2 fusion.91
  196.8 1.0 fusion.79
  197.8 1.0 fusion.3
  198.8 1.0 convolution_subtract_fusion
  199.8 1.0 convolution_add_fusion
  206.8 1.2 multiply_add_fusion.15
  214.7 0.8 pad_maximum_fusion.11
  215.5 1.9 collective-permute-start.7
  222.9 4.2 %collective-permute-done.7 = f32[2,256,256]{2,1,0:T(8,128)} collective-permute-done((f32[2,256,256]{2,1,0:T(8,128)}, f32[2,256,256]{2,1,0:T(8,128)}, u32[]{:S(2)}, u32[]{:S(2)}) %collective-permute-start.7) | collective-permute-done | bytes 524320 | tf_op jit(solution)/shard_map/ppermute | solution.py:20
  227.1 1.1 broadcast_select_fusion.3
  241.3 1.9 collective-permute-start.8
  243.7 8.1 %collective-permute-done.8 = f32[2,256,256]{2,1,0:T(8,128)S(1)} collective-permute-done((f32[2,256,256]{2,1,0:T(8,128)S(1)}, f32[2,256,256]{2,1,0:T(8,128)S(1)}, u32[]{:S(2)}, u32[]{:S(2)}) %collective-permute-start.8) | collective-permute-done | bytes 524320 | tf_op jit(solution)/shard_map/ppermute | solution.py:20
  264.9 1.9 collective-permute-start.9
  267.2 8.2 %collective-permute-done.9 = f32[2,256,256]{2,1,0:T(8,128)S(1)} collective-permute-done((f32[2,256,256]{2,1,0:T(8,128)S(1)}, f32[2,256,256]{2,1,0:T(8,128)S(1)}, u32[]{:S(2)}, u32[]{:S(2)}) %collective-permute-start.9) | collective-permute-done | bytes 524320 | tf_op jit(solution)/shard_map/ppermute | solution.py:20
  287.8 0.8 fusion.7
  288.6 1.9 collective-permute-start.10
  290.9 8.2 %collective-permute-done.10 = f32[2,256,256]{2,1,0:T(8,128)S(1)} collective-permute-done((f32[2,256,256]{2,1,0:T(8,128)S(1)}, f32[2,256,256]{2,1,0:T(8,128)S(1)}, u32[]{:S(2)}, u32[]{:S(2)}) %collective-permute-start.10) | collective-permute-done | bytes 524320 | tf_op jit(solution)/shard_map/ppermute | solution.py:20
  307.9 1.2 constant_dynamic-slice_fusion
  309.1 1.1 collective-permute-start.12
  310.2 1.2 constant_dynamic-slice_fusion.2
  311.4 1.6 collective-permute-start.11
  318.0 19.1 %collective-permute-done.12 = f32[2,2,256,256]{3,2,1,0:T(8,128)S(1)} collective-permute-done((f32[2,2,256,256]{3,2,1,0:T(8,128)}, f32[2,2,256,256]{3,2,1,0:T(8,128)S(1)}, u32[]{:S(2)}, u32[]{:S(2)}) %collective-permute-start.12) | collective-permute-done | bytes 1048608 | tf_op jit(solution)/shard_map/ppermute | solution.py:14
  337.1 15.6 %collective-permute-done.11 = f32[2,2,256,256]{3,2,1,0:T(8,128)} collective-permute-done((f32[2,2,256,256]{3,2,1,0:T(8,128)}, f32[2,2,256,256]{3,2,1,0:T(8,128)}, u32[]{:S(2)}, u32[]{:S(2)}) %collective-permute-start.11) | collective-permute-done | bytes 1048608 | tf_op jit(solution)/shard_map/ppermute | solution.py:14
  352.7 7.6 %fusion.2 = f32[2,2,256,1024]{3,2,1,0:T(8,128)} fusion(s32[]{:T(128)S(6)} %select_n.189, f32[2,2,256,256]{3,2,1,0:T(8,128)S(1)} %get-tuple-element.58, s32[]{:T(128)S(6)} %select_n.191, f32[2,2,256,256]{3,2,1,0:T(8,128)} %collective-permute-done.11, s32[]{:T(128)S(6)} %select_n.194, f32[2,2,256,256]{3,2,1,0:T(8,128)S(1)} %get-tuple-element.56, ...), kind=kLoop, calls=%fused_computation.30 | loop fusion | flops 3145728 | bytes 8388624 | tf_op jit(solution)/shard_map/add | solution.py:196
  (462 shorter events, 124.3 us)
Async XLA Ops:
  0.0 9.0 %copy-start.50 = (s32[2,2]{1,0:T(2,128)S(1)}, s32[2,2]{1,0:T(2,128)}, u32[]{:S(2)}) copy-start(s32[2,2]{1,0:T(2,128)} %param.7) | copy-start | bytes 52
  0.0 12.3 %copy-start.47 = (f32[2,256,256]{2,1,0:T(8,128)S(1)}, f32[2,256,256]{2,1,0:T(8,128)}, u32[]{:S(2)}) copy-start(f32[2,256,256]{2,1,0:T(8,128)} %param.5) | copy-start | bytes 1572868
  0.0 16.0 %collective-permute-start = (s32[2,2]{1,0:T(2,128)}, s32[2,2]{1,0:T(2,128)S(1)}, u32[]{:S(2)}, u32[]{:S(2)}) collective-permute-start(s32[2,2]{1,0:T(2,128)} %param.7), channel_id=1, source_target_pairs={{12,0},{0,4},{4,8},{8,12},{13,1},{1,5},{5,9},{9,13},{14,2},{2,6},{... | collective-permute-start | bytes 56 | tf_op jit(solution)/shard_map/ppermute | solution.py:14
  25.8 24.0 %collective-permute-start.2 = (f32[2,2,256,256]{3,2,1,0:T(8,128)S(1)}, f32[2,2,256,256]{3,2,1,0:T(8,128)}, u32[]{:S(2)}, u32[]{:S(2)}) collective-permute-start(f32[2,2,256,256]{3,2,1,0:T(8,128)S(1)} %get-tuple-element.51), channel_id=1, source_target_pairs={{4,0},{8,4},{12,8},{0,12},{5,1},{9,5},{13,9},{1,13},{6,2},{10,6},{... | collective-permute-start | bytes 3145736 | tf_op jit(solution)/shard_map/ppermute | solution.py:14
  32.6 17.3 %copy-start.6 = (f32[2,2,256,256]{3,2,1,0:T(8,128)S(1)}, f32[2,2,256,256]{3,2,1,0:T(8,128)}, u32[]{:S(2)}) copy-start(f32[2,2,256,256]{3,2,1,0:T(8,128)} %get-tuple-element.54) | copy-start | bytes 3145732
  32.6 39.8 %copy-start.5 = (f32[2,2,256,256]{3,2,1,0:T(8,128)S(1)}, f32[2,2,256,256]{3,2,1,0:T(8,128)}, u32[]{:S(2)}) copy-start(f32[2,2,256,256]{3,2,1,0:T(8,128)} %get-tuple-element.53) | copy-start | bytes 3145732
  32.6 39.8 %collective-permute-start.1 = (f32[2,2,256,256]{3,2,1,0:T(8,128)}, f32[2,2,256,256]{3,2,1,0:T(8,128)S(1)}, u32[]{:S(2)}, u32[]{:S(2)}) collective-permute-start(f32[2,2,256,256]{3,2,1,0:T(8,128)} %get-tuple-element.52), channel_id=1, source_target_pairs={{4,0},{8,4},{12,8},{0,12},{5,1},{9,5},{13,9},{1,13},{6,2},{10,6},{... | collective-permute-start | bytes 3145736 | tf_op jit(solution)/shard_map/ppermute | solution.py:14
  72.7 2.7 copy-start
  81.9 0.7 copy-start.29
  82.3 0.7 copy-start.31
  83.8 11.0 %collective-permute-start.3 = (f32[2,256,256]{2,1,0:T(8,128)}, f32[2,256,256]{2,1,0:T(8,128)S(1)}, u32[]{:S(2)}, u32[]{:S(2)}) collective-permute-start(f32[2,256,256]{2,1,0:T(8,128)} %pad_maximum_fusion.7), channel_id=1, source_target_pairs={{0,1},{1,2},{2,3},{4,5},{5,6},{6,7},{8,9},{9,10},{10,11},{12,13},{... | collective-permute-start | bytes 1572872 | tf_op jit(solution)/shard_map/ppermute | solution.py:20
  98.3 2.8 copy-start.4
  101.1 2.5 copy-start.11
  107.1 13.4 %copy-start.25 = (f32[256,256]{1,0:T(8,128)}, f32[256,256]{1,0:T(8,128)S(1)}, u32[]{:S(2)}) copy-start(f32[256,256]{1,0:T(8,128)S(1)} %convolution_subtract_fusion.64) | copy-start | bytes 786436
  107.5 13.4 %copy-start.27 = (f32[256,256]{1,0:T(8,128)}, f32[256,256]{1,0:T(8,128)S(1)}, u32[]{:S(2)}) copy-start(f32[256,256]{1,0:T(8,128)S(1)} %convolution_add_fusion.64) | copy-start | bytes 786436
  107.8 10.4 %collective-permute-start.4 = (f32[2,256,256]{2,1,0:T(8,128)S(1)}, f32[2,256,256]{2,1,0:T(8,128)S(1)}, u32[]{:S(2)}, u32[]{:S(2)}) collective-permute-start(f32[2,256,256]{2,1,0:T(8,128)S(1)} %pad_maximum_fusion.8), channel_id=1, source_target_pairs={{0,1},{1,2},{2,3},{4,5},{5,6},{6,7},{8,9},{9,10},{10,11},{12,13},{... | collective-permute-start | bytes 1572872 | tf_op jit(solution)/shard_map/ppermute | solution.py:20
  121.8 2.8 copy-start.3
  124.1 2.5 copy-start.13
  124.5 2.5 copy-start.15
  130.6 13.8 %copy-start.35 = (f32[256,256]{1,0:T(8,128)}, f32[256,256]{1,0:T(8,128)S(1)}, u32[]{:S(2)}) copy-start(f32[256,256]{1,0:T(8,128)S(1)} %convolution_subtract_fusion.56) | copy-start | bytes 786436
  131.0 13.8 %copy-start.37 = (f32[256,256]{1,0:T(8,128)}, f32[256,256]{1,0:T(8,128)S(1)}, u32[]{:S(2)}) copy-start(f32[256,256]{1,0:T(8,128)S(1)} %convolution_add_fusion.56) | copy-start | bytes 786436
  131.5 10.5 %collective-permute-start.5 = (f32[2,256,256]{2,1,0:T(8,128)S(1)}, f32[2,256,256]{2,1,0:T(8,128)S(1)}, u32[]{:S(2)}, u32[]{:S(2)}) collective-permute-start(f32[2,256,256]{2,1,0:T(8,128)S(1)} %pad_maximum_fusion.9), channel_id=1, source_target_pairs={{0,1},{1,2},{2,3},{4,5},{5,6},{6,7},{8,9},{9,10},{10,11},{12,13},{... | collective-permute-start | bytes 1572872 | tf_op jit(solution)/shard_map/ppermute | solution.py:20
  145.6 2.8 copy-start.2
  147.9 2.5 copy-start.17
  148.3 2.5 copy-start.19
  154.4 0.7 copy-start.39
  154.8 0.7 copy-start.41
  156.4 10.8 %collective-permute-start.6 = (f32[2,256,256]{2,1,0:T(8,128)}, f32[2,256,256]{2,1,0:T(8,128)}, u32[]{:S(2)}, u32[]{:S(2)}) collective-permute-start(f32[2,256,256]{2,1,0:T(8,128)} %get-tuple-element.148), channel_id=1, source_target_pairs={{0,1},{1,2},{2,3},{4,5},{5,6},{6,7},{8,9},{9,10},{10,11},{12,13},{... | collective-permute-start | bytes 1572872 | tf_op jit(solution)/shard_map/ppermute | solution.py:20
  174.5 2.8 copy-start.1
  176.9 2.5 copy-start.21
  177.3 2.5 copy-start.23
  183.8 3.6 copy-start.43
  184.2 3.2 copy-start.45
  186.3 5.1 %copy-start.49 = (f32[2,256,256]{2,1,0:T(8,128)S(1)}, f32[2,256,256]{2,1,0:T(8,128)}, u32[]{:S(2)}) copy-start(f32[2,256,256]{2,1,0:T(8,128)} %param.9) | copy-start | bytes 1572868
  206.8 4.3 %copy-start.33 = (f32[256,256]{1,0:T(8,128)}, f32[256,256]{1,0:T(8,128)S(1)}, u32[]{:S(2)}) copy-start(f32[256,256]{1,0:T(8,128)S(1)} %convolution_add_fusion.36) | copy-start | bytes 786436
  211.6 11.2 %copy-start.30 = (f32[256,256]{1,0:T(8,128)S(1)}, f32[256,256]{1,0:T(8,128)}, u32[]{:S(2)}) copy-start(f32[256,256]{1,0:T(8,128)} %copy-done.29) | copy-start | bytes 786436
  211.6 11.2 %copy-start.32 = (f32[256,256]{1,0:T(8,128)S(1)}, f32[256,256]{1,0:T(8,128)}, u32[]{:S(2)}) copy-start(f32[256,256]{1,0:T(8,128)} %copy-done.31) | copy-start | bytes 786436
  215.5 11.6 %collective-permute-start.7 = (f32[2,256,256]{2,1,0:T(8,128)}, f32[2,256,256]{2,1,0:T(8,128)}, u32[]{:S(2)}, u32[]{:S(2)}) collective-permute-start(f32[2,256,256]{2,1,0:T(8,128)} %pad_maximum_fusion.11), channel_id=1, source_target_pairs={{1,0},{2,1},{3,2},{5,4},{6,5},{7,6},{9,8},{10,9},{11,10},{13,12},{... | collective-permute-start | bytes 1572872 | tf_op jit(solution)/shard_map/ppermute | solution.py:20
  222.7 5.5 %copy-start.9 = (f32[1,2,2,256,256]{4,3,2,1,0:T(8,128)S(1)}, f32[1,2,2,256,256]{4,3,2,1,0:T(8,128)}, u32[]{:S(2)}) copy-start(f32[1,2,2,256,256]{4,3,2,1,0:T(8,128)} %get-tuple-element.67) | copy-start | bytes 3145732
  237.8 5.4 %copy-start.26 = (f32[256,256]{1,0:T(8,128)S(1)}, f32[256,256]{1,0:T(8,128)}, u32[]{:S(2)}) copy-start(f32[256,256]{1,0:T(8,128)} %copy-done.25) | copy-start | bytes 786436
  237.8 5.4 %copy-start.28 = (f32[256,256]{1,0:T(8,128)S(1)}, f32[256,256]{1,0:T(8,128)}, u32[]{:S(2)}) copy-start(f32[256,256]{1,0:T(8,128)} %copy-done.27) | copy-start | bytes 786436
  238.2 5.1 %copy-start.36 = (f32[256,256]{1,0:T(8,128)S(1)}, f32[256,256]{1,0:T(8,128)}, u32[]{:S(2)}) copy-start(f32[256,256]{1,0:T(8,128)} %copy-done.35) | copy-start | bytes 786436
  238.2 5.1 %copy-start.38 = (f32[256,256]{1,0:T(8,128)S(1)}, f32[256,256]{1,0:T(8,128)}, u32[]{:S(2)}) copy-start(f32[256,256]{1,0:T(8,128)} %copy-done.37) | copy-start | bytes 786436
  239.0 4.4 %copy-start.40 = (f32[256,256]{1,0:T(8,128)S(1)}, f32[256,256]{1,0:T(8,128)}, u32[]{:S(2)}) copy-start(f32[256,256]{1,0:T(8,128)} %copy-done.39) | copy-start | bytes 786436
  239.0 4.4 %copy-start.42 = (f32[256,256]{1,0:T(8,128)S(1)}, f32[256,256]{1,0:T(8,128)}, u32[]{:S(2)}) copy-start(f32[256,256]{1,0:T(8,128)} %copy-done.41) | copy-start | bytes 786436
  239.4 4.0 %copy-start.12 = (f32[256,256]{1,0:T(8,128)S(1)}, f32[256,256]{1,0:T(8,128)}, u32[]{:S(2)}) copy-start(f32[256,256]{1,0:T(8,128)} %copy-done.11) | copy-start | bytes 786436
  239.4 4.0 %copy-start.14 = (f32[256,256]{1,0:T(8,128)S(1)}, f32[256,256]{1,0:T(8,128)}, u32[]{:S(2)}) copy-start(f32[256,256]{1,0:T(8,128)} %copy-done.13) | copy-start | bytes 786436
  239.4 4.0 %copy-start.16 = (f32[256,256]{1,0:T(8,128)S(1)}, f32[256,256]{1,0:T(8,128)}, u32[]{:S(2)}) copy-start(f32[256,256]{1,0:T(8,128)} %copy-done.15) | copy-start | bytes 786436
  239.4 4.0 %copy-start.18 = (f32[256,256]{1,0:T(8,128)S(1)}, f32[256,256]{1,0:T(8,128)}, u32[]{:S(2)}) copy-start(f32[256,256]{1,0:T(8,128)} %copy-done.17) | copy-start | bytes 786436
  239.5 4.0 %copy-start.20 = (f32[256,256]{1,0:T(8,128)S(1)}, f32[256,256]{1,0:T(8,128)}, u32[]{:S(2)}) copy-start(f32[256,256]{1,0:T(8,128)} %copy-done.19) | copy-start | bytes 786436
  239.5 4.0 %copy-start.22 = (f32[256,256]{1,0:T(8,128)S(1)}, f32[256,256]{1,0:T(8,128)}, u32[]{:S(2)}) copy-start(f32[256,256]{1,0:T(8,128)} %copy-done.21) | copy-start | bytes 786436
  239.5 4.0 %copy-start.24 = (f32[256,256]{1,0:T(8,128)S(1)}, f32[256,256]{1,0:T(8,128)}, u32[]{:S(2)}) copy-start(f32[256,256]{1,0:T(8,128)} %copy-done.23) | copy-start | bytes 786436
  241.3 10.5 %collective-permute-start.8 = (f32[2,256,256]{2,1,0:T(8,128)S(1)}, f32[2,256,256]{2,1,0:T(8,128)S(1)}, u32[]{:S(2)}, u32[]{:S(2)}) collective-permute-start(f32[2,256,256]{2,1,0:T(8,128)S(1)} %pad_maximum_fusion.12), channel_id=1, source_target_pairs={{1,0},{2,1},{3,2},{5,4},{6,5},{7,6},{9,8},{10,9},{11,10},{13,12},{... | collective-permute-start | bytes 1572872 | tf_op jit(solution)/shard_map/ppermute | solution.py:20
  243.3 8.6 %copy-start.8 = (f32[1,2,2,256,256]{4,3,2,1,0:T(8,128)S(1)}, f32[1,2,2,256,256]{4,3,2,1,0:T(8,128)}, u32[]{:S(2)}) copy-start(f32[1,2,2,256,256]{4,3,2,1,0:T(8,128)} %get-tuple-element.68) | copy-start | bytes 3145732
  261.5 5.3 %copy-start.44 = (f32[256,256]{1,0:T(8,128)S(1)}, f32[256,256]{1,0:T(8,128)}, u32[]{:S(2)}) copy-start(f32[256,256]{1,0:T(8,128)} %copy-done.43) | copy-start | bytes 786436
  261.5 5.3 %copy-start.46 = (f32[256,256]{1,0:T(8,128)S(1)}, f32[256,256]{1,0:T(8,128)}, u32[]{:S(2)}) copy-start(f32[256,256]{1,0:T(8,128)} %copy-done.45) | copy-start | bytes 786436
  264.9 10.5 %collective-permute-start.9 = (f32[2,256,256]{2,1,0:T(8,128)S(1)}, f32[2,256,256]{2,1,0:T(8,128)S(1)}, u32[]{:S(2)}, u32[]{:S(2)}) collective-permute-start(f32[2,256,256]{2,1,0:T(8,128)S(1)} %pad_maximum_fusion.13), channel_id=1, source_target_pairs={{1,0},{2,1},{3,2},{5,4},{6,5},{7,6},{9,8},{10,9},{11,10},{13,12},{... | collective-permute-start | bytes 1572872 | tf_op jit(solution)/shard_map/ppermute | solution.py:20
  266.8 8.6 %copy-start.7 = (f32[1,2,2,256,256]{4,3,2,1,0:T(8,128)S(1)}, f32[1,2,2,256,256]{4,3,2,1,0:T(8,128)}, u32[]{:S(2)}) copy-start(f32[1,2,2,256,256]{4,3,2,1,0:T(8,128)} %get-tuple-element.65) | copy-start | bytes 3145732
  288.6 10.5 %collective-permute-start.10 = (f32[2,256,256]{2,1,0:T(8,128)S(1)}, f32[2,256,256]{2,1,0:T(8,128)S(1)}, u32[]{:S(2)}, u32[]{:S(2)}) collective-permute-start(f32[2,256,256]{2,1,0:T(8,128)S(1)} %pad_maximum_fusion.14), channel_id=1, source_target_pairs={{1,0},{2,1},{3,2},{5,4},{6,5},{7,6},{9,8},{10,9},{11,10},{13,12},{... | collective-permute-start | bytes 1572872 | tf_op jit(solution)/shard_map/ppermute | solution.py:20
  290.5 8.6 %copy-start.10 = (f32[1,2,2,256,256]{4,3,2,1,0:T(8,128)S(1)}, f32[1,2,2,256,256]{4,3,2,1,0:T(8,128)}, u32[]{:S(2)}) copy-start(f32[1,2,2,256,256]{4,3,2,1,0:T(8,128)} %get-tuple-element.59) | copy-start | bytes 3145732
  304.0 1.9 copy-start.34
  304.0 1.9 copy-start.48
  309.1 28.0 %collective-permute-start.12 = (f32[2,2,256,256]{3,2,1,0:T(8,128)}, f32[2,2,256,256]{3,2,1,0:T(8,128)S(1)}, u32[]{:S(2)}, u32[]{:S(2)}) collective-permute-start(f32[2,2,256,256]{3,2,1,0:T(8,128)} %get-tuple-element.55), channel_id=1, source_target_pairs={{12,0},{0,4},{4,8},{8,12},{13,1},{1,5},{5,9},{9,13},{14,2},{2,6},{... | collective-permute-start | bytes 3145736 | tf_op jit(solution)/shard_map/ppermute | solution.py:14
  311.4 41.3 %collective-permute-start.11 = (f32[2,2,256,256]{3,2,1,0:T(8,128)}, f32[2,2,256,256]{3,2,1,0:T(8,128)}, u32[]{:S(2)}, u32[]{:S(2)}) collective-permute-start(f32[2,2,256,256]{3,2,1,0:T(8,128)} %get-tuple-element.57), channel_id=1, source_target_pairs={{12,0},{0,4},{4,8},{8,12},{13,1},{1,5},{5,9},{9,13},{14,2},{2,6},{... | collective-permute-start | bytes 3145736 | tf_op jit(solution)/shard_map/ppermute | solution.py:14
